TPU v7x, 128 devices: a whole 4x4x4 slice. The times are simulated.
128 devices in a mesh: fold: 16 (over x, z), blk: 8 (over y, core).
Axes of the slice: x: 4, y: 4, z: 4, core: 2. Of those that a mesh axis runs over, the one named last changes fastest.
Arguments:
- genotypes: bfloat16 [131072, 8192], P('fold', 'blk'), may hold values from 0 to 2, as said below
- phenotypes: bfloat16 [32, 131072], P(None, 'fold'), may hold values from -4 to 4
- trait_order: int32 [32], replicated, may hold values from 0 to 31, each once
Outputs:
- predict: float32 [32, 131072], P('blk', 'fold')
Inputs may be any that keep to these rules, and one draw needn't show every extreme that they name: `genotypes`: dosages are 0, 1 or 2. `trait_order`: a permutation of the 32 traits.
All inputs are finite; a program needn't handle non-finite values.
Results may differ from a plain program's by a relative error of at most 0.00235.
Values may be sent and summed in bfloat16 or wider, within the bound.
No kernel may reach another device: no remote copies, remote signals or barrier semaphores. Data moves between devices by JAX's collectives and lax.ppermute only.
A program may use at most 320 MiB of HBM per device.

v0:
```python
import jax
import jax.numpy as jnp
from jax import lax
from jax.experimental import pallas as pl
from jax.sharding import PartitionSpec as P

B = 512
ITERS = 8


LAMBDAS = (0.2, 2.0)
LEVEL_ONE = 0.1
EPSILON = 1e-06


def chebyshev(times_system, target, low_edge, high_edge):
    center = 0.5 * (high_edge + low_edge)
    radius = 0.5 * (high_edge - low_edge)
    sigma_ratio = center / radius
    rho_now = 1.0 / sigma_ratio
    direction = target / center
    solution = jnp.zeros_like(target)
    residual = target
    for iteration in range(ITERS):
        solution = solution + direction
        if iteration + 1 < ITERS:
            residual = residual - times_system(direction)
            rho_next = 1.0 / (2.0 * sigma_ratio - rho_now)
            direction = rho_next * rho_now * direction + 2.0 * rho_next / radius * residual
            rho_now = rho_next
    return solution


def _spd_solve_kernel(a_ref, b_ref, w_ref):
    a = a_ref[...]
    b = b_ref[...]
    t, q, _ = a.shape
    rowi = lax.broadcasted_iota(jnp.int32, (t, q, 1), 1)
    coli = lax.broadcasted_iota(jnp.int32, (t, 1, q), 2)
    y = jnp.zeros_like(b)
    columns = []
    for k in range(q):
        s = jnp.sqrt(a[:, k:k + 1, k:k + 1])
        lcol = jnp.where(rowi == k, s, jnp.where(rowi > k, a[:, :, k:k + 1] / s, 0.0))
        lrow = jnp.where(coli == k, s, jnp.where(coli > k, a[:, k:k + 1, :] / s, 0.0))
        a = a - lcol * lrow
        yk = b[:, k:k + 1, :] / s
        b = b - jnp.where(rowi > k, lcol * yk, 0.0)
        y = jnp.where(rowi == k, yk, y)
        columns.append(lcol)
    w = jnp.zeros_like(b)
    for k in reversed(range(q)):
        lcol = columns[k]
        acc = jnp.sum(jnp.where(rowi > k, lcol * w, 0.0), axis=1, keepdims=True)
        w = jnp.where(rowi == k, (y[:, k:k + 1, :] - acc) / lcol[:, k:k + 1, :], w)
    w_ref[...] = w


def spd_solve(a, b):
    return pl.pallas_call(
        _spd_solve_kernel,
        out_shape=jax.ShapeDtypeStruct(b.shape, jnp.float32),
    )(a, b)


def butterfly_sum(x, axis):
    n = lax.axis_size(axis)
    if n & (n - 1):
        return lax.psum(x, axis)
    stride = 1
    while stride < n:
        radix = min(4, n // stride)
        total = x
        for shift in range(1, radix):
            perm = []
            for i in range(n):
                digit = (i // stride) % radix
                perm.append((i, i + ((digit + shift) % radix - digit) * stride))
            total = total + lax.ppermute(x, axis, perm)
        x = total
        stride *= radix
    return x


def exchange_sum(arrays, axis):
    n = lax.axis_size(axis)
    flat = jnp.concatenate([a.reshape(-1) for a in arrays])
    size = flat.shape[0]
    unit = n * 8 * 128
    flat = jnp.pad(flat, (0, -(-size // unit) * unit - size))
    pieces = lax.all_to_all(flat.reshape(n, -1, 128), axis, 0, 0, tiled=True)
    chunk = jnp.sum(pieces, axis=0)
    whole = lax.all_to_all(jnp.broadcast_to(chunk[None], (n,) + chunk.shape), axis, 0, 0, tiled=True)
    whole = whole.reshape(-1)
    out = []
    offset = 0
    for a in arrays:
        out.append(whole[offset:offset + a.size].reshape(a.shape))
        offset += a.size
    return out


def per_device(genotypes, phenotypes, trait_order):
    n_fold = lax.axis_size("fold")
    sample_rows = genotypes.shape[0]
    block_count = genotypes.shape[1] // B
    total_rows = sample_rows * n_fold
    held_rows = float(total_rows - sample_rows)
    phen = jnp.take(phenotypes, trait_order, axis=0)
    p_size = phen.shape[0]
    half = B // 2
    rows = lax.broadcasted_iota(jnp.int32, (half, half), 0)
    cols = lax.broadcasted_iota(jnp.int32, (half, half), 1)
    eye_h = rows == cols

    def pack(gram):
        a11, a12, a22 = gram[:half, :half], gram[:half, half:], gram[half:, half:]
        tile = jnp.where(rows > cols, a11, a22)
        diag = jnp.sum(jnp.where(eye_h, a11, 0.0), axis=1)
        return jnp.concatenate([a12, tile, diag[None]], axis=0)

    def unpack(packed):
        a12, tile, diag = packed[:half], packed[half:B], packed[B]
        tile_t = tile.T
        a22 = jnp.where(rows <= cols, tile, tile_t)
        a11 = jnp.where(rows > cols, tile, jnp.where(rows < cols, tile_t, jnp.where(eye_h, diag[:, None], 0.0)))
        top = jnp.concatenate([a11, a12], axis=1)
        bottom = jnp.concatenate([a12.T, a22], axis=1)
        return jnp.concatenate([top, bottom], axis=0)

    gram_parts = []
    early_totals = []
    for b in range(block_count):
        xb = genotypes[:, b * B:(b + 1) * B]
        gram_parts.append(jnp.einsum("si,sj->ij", xb, xb, preferred_element_type=jnp.float32))
        if b + 1 < block_count:
            early_totals += exchange_sum([pack(gram_parts[-1])], "fold")
    phen_aug = jnp.concatenate([phen, jnp.ones((1, sample_rows), phen.dtype)], axis=0)
    cross_aug = jnp.dot(phen_aug, genotypes, preferred_element_type=jnp.float32)
    phen_local = jnp.sum(phen.astype(jnp.float32), axis=1)
    phen_row = jnp.zeros((1, genotypes.shape[1]), jnp.float32).at[0, :p_size].set(phen_local)
    sums_local = jnp.concatenate([cross_aug, phen_row], axis=0)
    totals = early_totals + exchange_sum([pack(gram_parts[-1]), sums_local], "fold")
    sums_total = totals[-1]
    gram_part = jnp.stack(gram_parts)
    gram_sum = jnp.stack([unpack(p) for p in totals[:-1]])
    phen_total = sums_total[p_size + 1, :p_size]
    cross_aug = cross_aug.reshape(p_size + 1, block_count, B)
    cross_aug_total = sums_total[: p_size + 1].reshape(p_size + 1, block_count, B)
    cross_local = jnp.transpose(cross_aug[:p_size], (1, 0, 2))
    col_local = cross_aug[p_size]
    cross_total = jnp.transpose(cross_aug_total[:p_size], (1, 0, 2))
    col_total = cross_aug_total[p_size]
    mean_dose = col_total / total_rows
    eye = jnp.eye(B, dtype=jnp.bool_)
    gram_diag = jnp.sum(jnp.where(eye[None], gram_sum, 0.0), axis=2)
    inv_scale = 1.0 / jnp.sqrt(gram_diag / total_rows - mean_dose * mean_dose + EPSILON)
    gram_out = gram_sum - gram_part
    col_out = col_total - col_local
    cross_out = cross_total - cross_local
    phen_out = phen_total - phen_local
    centered = (
        gram_out
        - col_out[:, :, None] * mean_dose[:, None, :]
        - mean_dose[:, :, None] * col_out[:, None, :]
        + held_rows * mean_dose[:, :, None] * mean_dose[:, None, :]
    )
    system = inv_scale[:, :, None] * centered * inv_scale[:, None, :] / held_rows
    target = (
        (cross_out - phen_out[None, :, None] * mean_dose[:, None, :])
        * inv_scale[:, None, :]
        / held_rows
    )
    bound = jnp.max(jnp.sum(jnp.abs(system), axis=2), axis=1)
    penalty = jnp.array(LAMBDAS, jnp.float32)
    low_edge = jnp.broadcast_to(penalty[None, :, None, None], (block_count, penalty.shape[0], 1, 1))
    high_edge = low_edge + bound[:, None, None, None]

    def times_system(direction):
        return (
            jnp.einsum(
                "brpi,bij->brpj",
                direction,
                system,
                precision=lax.Precision.HIGHEST,
                preferred_element_type=jnp.float32,
            )
            + low_edge * direction
        )

    stacked = jnp.broadcast_to(target[:, None], (block_count, penalty.shape[0]) + target.shape[1:])
    coef = chebyshev(times_system, stacked, low_edge, high_edge)
    scaled = (inv_scale[:, None, None, :] * coef).astype(jnp.bfloat16)
    offset = jnp.einsum(
        "bi,brpi->pbr", mean_dose, scaled.astype(jnp.float32), precision=lax.Precision.HIGHEST
    )
    halves = 2
    part_rows = sample_rows // halves
    blk_index = lax.axis_index("blk")
    level_parts = []
    hgram_own = 0.0
    hcross_own = 0.0
    for h in range(halves):
        rows_h = slice(h * part_rows, (h + 1) * part_rows)
        product = jnp.stack(
            [
                jnp.einsum(
                    "si,rpi->prs",
                    genotypes[rows_h, b * B:(b + 1) * B],
                    scaled[b],
                    preferred_element_type=jnp.float32,
                )
                for b in range(block_count)
            ],
            axis=1,
        )
        feature = (product - offset[:, :, :, None]).astype(jnp.bfloat16)
        owned = lax.all_to_all(feature, "blk", split_axis=0, concat_axis=1, tiled=True)
        own_traits = owned.shape[0]
        feature_count = owned.shape[1] * owned.shape[2]
        level_feat = owned.reshape(own_traits, feature_count, part_rows)
        target_own = lax.dynamic_slice_in_dim(phen[:, rows_h], blk_index * own_traits, own_traits, 0)
        hgram_own = hgram_own + jnp.einsum(
            "pqs,pts->pqt", level_feat, level_feat, preferred_element_type=jnp.float32
        )
        hcross_own = hcross_own + jnp.einsum(
            "pqs,ps->pq", level_feat, target_own, preferred_element_type=jnp.float32
        )
        level_parts.append(level_feat)
    level_own = jnp.concatenate([hgram_own, hcross_own[:, :, None]], axis=2)
    level_total = butterfly_sum(level_own, "fold")
    hgram_total = level_total[:, :, :feature_count]
    hcross_total = level_total[:, :, feature_count]
    hgram_out = hgram_total - hgram_own
    hcross_out = hcross_total - hcross_own
    trace_sum = jnp.trace(hgram_out, axis1=1, axis2=2)
    level_system = hgram_out / held_rows + (LEVEL_ONE * trace_sum / (held_rows * feature_count))[
        :, None, None
    ] * jnp.eye(feature_count, dtype=jnp.float32)
    weight = spd_solve(level_system, (hcross_out / held_rows)[:, :, None])[:, :, 0]
    return jnp.concatenate(
        [
            jnp.einsum("pq,pqs->ps", weight, f.astype(jnp.float32), precision=lax.Precision.HIGHEST)
            for f in level_parts
        ],
        axis=1,
    )


def solution(mesh):
    return jax.shard_map(
        per_device,
        mesh=mesh,
        in_specs=(P("fold", "blk"), P(None, "fold"), P()),
        out_specs=P("blk", "fold"),
        check_vma=False,
    )
```

profile of v0, /device:TPU:0, one launch (start us, length us, event | category | flops | bytes accessed | tf_op | source)
XLA Modules:
  0.0 213.1 jit_solution(5152011181785531342)
XLA Ops:
  0.0 9.9 %fusion.2 = f32[512,512]{1,0:T(8,128)S(1)} fusion(bf16[8192,1024]{1,0:T(8,128)(2,1)} %param.6), kind=kOutput, calls=%fused_computation.3 | convolution fusion | flops 4294967296 | bytes 9437184 | tf_op jit(solution)/shard_map/si,sj->ij/dot_general | solution.py:135
  12.0 8.0 %all-to-all-start = ((f32[16,72,128]{2,1,0:T(8,128)}), f32[16,72,128]{2,1,0:T(8,128)S(1)}, u32[]{:S(2)}, u32[]{:S(2)}) async-start(f32[16,72,128]{2,1,0:T(8,128)} %bitcast.1), calls=%async_computation | async-start | bytes 1179648 | tf_op jit(solution)/shard_map/all_to_all | solution.py:91
  20.6 10.0 %fusion = f32[512,512]{1,0:T(8,128)S(1)} fusion(bf16[8192,1024]{1,0:T(8,128)(2,1)} %param.6), kind=kOutput, calls=%fused_computation.1 | convolution fusion | flops 4294967296 | bytes 9437184 | tf_op jit(solution)/shard_map/si,sj->ij/dot_general | solution.py:135
  31.9 8.7 %fusion.91 = f32[33,1024]{1,0:T(8,128)S(1)} fusion(bf16[8192,1024]{1,0:T(8,128)(2,1)} %param.6, bf16[32,8192]{1,0:T(8,128)(2,1)S(1)} %get-tuple-element.20), kind=kOutput, calls=%fused_computation.73 | convolution fusion | flops 553648128 | bytes 17436672 | tf_op jit(solution)/shard_map/dot_general | solution.py:139
  42.5 7.2 %all-to-all-start.2 = ((f32[16,88,128]{2,1,0:T(8,128)}), f32[16,88,128]{2,1,0:T(8,128)S(1)}, u32[]{:S(2)}, u32[]{:S(2)}) async-start(f32[16,88,128]{2,1,0:T(8,128)} %bitcast.8), calls=%async_computation.2 | async-start | bytes 1441792 | tf_op jit(solution)/shard_map/all_to_all | solution.py:91
  49.8 13.0 %all-to-all-done.2 = f32[16,88,128]{2,1,0:T(8,128)S(1)} async-done(((f32[16,88,128]{2,1,0:T(8,128)}), f32[16,88,128]{2,1,0:T(8,128)S(1)}, u32[]{:S(2)}, u32[]{:S(2)}) %all-to-all-start.2) | async-done | bytes 720928 | tf_op jit(solution)/shard_map/all_to_all | solution.py:91
  63.7 3.7 %all-to-all-start.1 = ((f32[16,72,128]{2,1,0:T(8,128)}), f32[16,72,128]{2,1,0:T(8,128)S(1)}, u32[]{:S(2)}, u32[]{:S(2)}) async-start(f32[16,72,128]{2,1,0:T(8,128)} %broadcast_in_dim.113), calls=%async_computation.1 | async-start | bytes 1179648 | tf_op jit(solution)/shard_map/all_to_all | solution.py:93
  67.4 10.8 %all-to-all-done.1 = f32[16,72,128]{2,1,0:T(8,128)S(1)} async-done(((f32[16,72,128]{2,1,0:T(8,128)}), f32[16,72,128]{2,1,0:T(8,128)S(1)}, u32[]{:S(2)}, u32[]{:S(2)}) %all-to-all-start.1) | async-done | bytes 589856 | tf_op jit(solution)/shard_map/all_to_all | solution.py:93
  79.1 14.1 %all-to-all-start.3 = ((f32[16,88,128]{2,1,0:T(8,128)}), f32[16,88,128]{2,1,0:T(8,128)S(1)}, u32[]{:S(2)}, u32[]{:S(2)}) async-start(f32[16,88,128]{2,1,0:T(8,128)} %broadcast_in_dim.119), calls=%async_computation.3 | async-start | bytes 1441792 | tf_op jit(solution)/shard_map/all_to_all | solution.py:93
  96.6 7.5 %all-to-all-done.3 = f32[16,88,128]{2,1,0:T(8,128)S(1)} async-done(((f32[16,88,128]{2,1,0:T(8,128)}), f32[16,88,128]{2,1,0:T(8,128)S(1)}, u32[]{:S(2)}, u32[]{:S(2)}) %all-to-all-start.3) | async-done | bytes 720928 | tf_op jit(solution)/shard_map/all_to_all | solution.py:93
  109.4 2.6 %abs_reduce_fusion = (f32[2,512]{1,0:T(2,128)S(1)}, f32[2,512,512]{2,1,0:T(8,128)S(1)}) fusion(f32[2,512]{1,0:T(2,128)S(1)} %get-tuple-element.37, f32[2,512]{1,0:T(2,128)S(1)} %get-tuple-element.38, f32[2,512]{1,0:T(2,128)S(1)} %get-tuple-element.39, f32[2,512]{1,0:T(2,128)S(1)} %get-tuple-element.40, f32[1,512,512]{2,1,0:T(8,128)S(1)} %bitcast.201, ...), kind=kLoop, calls=%fused_computation.43 | loop fusion | flops 7339008 | bytes 6311936 | tf_op jit(solution)/shard_map/reduce_sum | solution.py:174
  115.3 1.5 multiply_add_fusion.2
  119.6 1.5 fusion.67
  121.1 1.7 fusion.88
  122.8 3.7 %convolution_bitcast_fusion = f32[32,1,2,4096]{3,0,2,1:T(8,128)S(1)} fusion(bf16[8192,1024]{1,0:T(8,128)(2,1)} %param.6, bf16[2,2,32,512]{3,2,1,0:T(8,128)(2,1)S(1)} %fusion.88), kind=kOutput, calls=%fused_computation.5 | convolution fusion | flops 268435456 | bytes 5308416 | tf_op jit(solution)/shard_map/si,rpi->prs/dot_general | solution.py:207
  126.5 3.6 %convolution_bitcast_fusion.1 = f32[32,1,2,4096]{3,0,2,1:T(8,128)S(1)} fusion(bf16[8192,1024]{1,0:T(8,128)(2,1)} %param.6, bf16[2,2,32,512]{3,2,1,0:T(8,128)(2,1)S(1)} %fusion.88), kind=kOutput, calls=%fused_computation.6 | convolution fusion | flops 268435456 | bytes 5308416 | tf_op jit(solution)/shard_map/si,rpi->prs/dot_general | solution.py:207
  133.8 2.1 copy.79
  135.9 4.5 %all-to-all-start.5 = ((bf16[32,2,2,4096]{3,2,1,0:T(2,128)(2,1)}), bf16[32,2,2,4096]{3,2,1,0:T(2,128)(2,1)S(1)}, u32[]{:S(2)}, u32[]{:S(2)}) async-start(bf16[32,2,2,4096]{3,2,1,0:T(2,128)(2,1)} %copy.79), calls=%async_computation.5 | async-start | bytes 2097152 | tf_op jit(solution)/shard_map/all_to_all | solution.py:218
  140.4 2.1 copy.77
  142.5 13.9 %all-to-all-done.5 = bf16[32,2,2,4096]{3,2,1,0:T(2,128)(2,1)S(1)} async-done(((bf16[32,2,2,4096]{3,2,1,0:T(2,128)(2,1)}), bf16[32,2,2,4096]{3,2,1,0:T(2,128)(2,1)S(1)}, u32[]{:S(2)}, u32[]{:S(2)}) %all-to-all-start.5) | async-done | bytes 1048608 | tf_op jit(solution)/shard_map/all_to_all | solution.py:218
  156.3 3.6 %all-to-all-start.4 = ((bf16[32,2,2,4096]{3,2,1,0:T(2,128)(2,1)}), bf16[32,2,2,4096]{3,2,1,0:T(2,128)(2,1)S(1)}, u32[]{:S(2)}, u32[]{:S(2)}) async-start(bf16[32,2,2,4096]{3,2,1,0:T(2,128)(2,1)} %copy.77), calls=%async_computation.4 | async-start | bytes 2097152 | tf_op jit(solution)/shard_map/all_to_all | solution.py:218
  160.0 2.1 copy.108
  162.1 1.5 reshape.899
  163.6 12.2 %all-to-all-done.4 = bf16[32,2,2,4096]{3,2,1,0:T(2,128)(2,1)S(1)} async-done(((bf16[32,2,2,4096]{3,2,1,0:T(2,128)(2,1)}), bf16[32,2,2,4096]{3,2,1,0:T(2,128)(2,1)S(1)}, u32[]{:S(2)}, u32[]{:S(2)}) %all-to-all-start.4) | async-done | bytes 1048608 | tf_op jit(solution)/shard_map/all_to_all | solution.py:218
  175.8 2.1 copy.109
  177.9 1.5 reshape.898
  182.2 2.3 %collective-permute-start.2 = (f32[4,32,33]{2,1,0:T(8,128)S(1)}, f32[4,32,33]{2,1,0:T(8,128)S(1)}, u32[]{:S(2)}, u32[]{:S(2)}) collective-permute-start(f32[4,32,33]{2,1,0:T(8,128)S(1)} %pad_maximum_fusion.4), channel_id=1, source_target_pairs={{0,24},{8,0},{16,8},{24,16},{32,56},{40,32},{48,40},{56,48},{64,88... | collective-permute-start | bytes 50696 | tf_op jit(solution)/shard_map/ppermute | solution.py:79
  184.5 3.2 %collective-permute-done.1 = f32[4,32,33]{2,1,0:T(8,128)S(1)} collective-permute-done((f32[4,32,33]{2,1,0:T(8,128)S(1)}, f32[4,32,33]{2,1,0:T(8,128)S(1)}, u32[]{:S(2)}, u32[]{:S(2)}) %collective-permute-start.1) | collective-permute-done | bytes 16928 | tf_op jit(solution)/shard_map/ppermute | solution.py:79
  187.7 2.3 %collective-permute-done = f32[4,32,33]{2,1,0:T(8,128)S(1)} collective-permute-done((f32[4,32,33]{2,1,0:T(8,128)S(1)}, f32[4,32,33]{2,1,0:T(8,128)S(1)}, u32[]{:S(2)}, u32[]{:S(2)}) %collective-permute-start) | collective-permute-done | bytes 16928 | tf_op jit(solution)/shard_map/ppermute | solution.py:79
  192.6 1.8 collective-permute-done.5
  194.4 2.5 %collective-permute-done.4 = f32[4,32,33]{2,1,0:T(8,128)S(1)} collective-permute-done((f32[4,32,33]{2,1,0:T(8,128)S(1)}, f32[4,32,33]{2,1,0:T(8,128)S(1)}, u32[]{:S(2)}, u32[]{:S(2)}) %collective-permute-start.4) | collective-permute-done | bytes 16928 | tf_op jit(solution)/shard_map/ppermute | solution.py:79
  199.3 10.5 %shard_map.46 = f32[4,32,1]{2,1,0:T(8,128)} custom-call(f32[4,32,32]{2,1,0:T(8,128)} %multiply_add_fusion.11.a_ref, f32[4,32,1]{2,1,0:T(8,128)} %copy.82.b_ref), custom_call_target="tpu_custom_call" | custom-call | tf_op jit(solution)/shard_map/pallas_call | solution.py:60
  (128 shorter events, 36.6 us)
Async XLA Ops:
  0.0 30.7 %copy-start = (bf16[32,8192]{1,0:T(8,128)(2,1)S(1)}, bf16[32,8192]{1,0:T(8,128)(2,1)}, u32[]{:S(2)}) copy-start(bf16[32,8192]{1,0:T(8,128)(2,1)} %param.7) | copy-start | bytes 1572868
  9.9 1.0 copy-start.2
  11.0 9.6 %copy-start.12 = (s32[32]{0:T(128)S(1)}, s32[32]{0:T(128)}, u32[]{:S(2)}) copy-start(s32[32]{0:T(128)} %param.8) | copy-start | bytes 388
  12.0 30.6 %all-to-all-start = ((f32[16,72,128]{2,1,0:T(8,128)}), f32[16,72,128]{2,1,0:T(8,128)S(1)}, u32[]{:S(2)}, u32[]{:S(2)}) async-start(f32[16,72,128]{2,1,0:T(8,128)} %bitcast.1), calls=%async_computation | async-start | bytes 1179648 | tf_op jit(solution)/shard_map/all_to_all | solution.py:91
  30.6 10.8 %copy-start.4 = (f32[512,512]{1,0:T(8,128)}, f32[512,512]{1,0:T(8,128)S(1)}, u32[]{:S(2)}) copy-start(f32[512,512]{1,0:T(8,128)S(1)} %fusion) | copy-start | bytes 3145732
  40.6 0.7 copy-start.6
  42.5 20.3 %all-to-all-start.2 = ((f32[16,88,128]{2,1,0:T(8,128)}), f32[16,88,128]{2,1,0:T(8,128)S(1)}, u32[]{:S(2)}, u32[]{:S(2)}) async-start(f32[16,88,128]{2,1,0:T(8,128)} %bitcast.8), calls=%async_computation.2 | async-start | bytes 1441792 | tf_op jit(solution)/shard_map/all_to_all | solution.py:91
  63.7 29.6 %copy-start.7 = (f32[33,1024]{1,0:T(8,128)S(1)}, f32[33,1024]{1,0:T(8,128)}, u32[]{:S(2)}) copy-start(f32[33,1024]{1,0:T(8,128)} %copy-done.6) | copy-start | bytes 405508
  63.7 14.5 %all-to-all-start.1 = ((f32[16,72,128]{2,1,0:T(8,128)}), f32[16,72,128]{2,1,0:T(8,128)S(1)}, u32[]{:S(2)}, u32[]{:S(2)}) async-start(f32[16,72,128]{2,1,0:T(8,128)} %broadcast_in_dim.113), calls=%async_computation.1 | async-start | bytes 1179648 | tf_op jit(solution)/shard_map/all_to_all | solution.py:93
  79.1 25.0 %all-to-all-start.3 = ((f32[16,88,128]{2,1,0:T(8,128)}), f32[16,88,128]{2,1,0:T(8,128)S(1)}, u32[]{:S(2)}, u32[]{:S(2)}) async-start(f32[16,88,128]{2,1,0:T(8,128)} %broadcast_in_dim.119), calls=%async_computation.3 | async-start | bytes 1441792 | tf_op jit(solution)/shard_map/all_to_all | solution.py:93
  96.6 12.2 %copy-start.1 = (f32[1,512,512]{2,1,0:T(8,128)}, f32[1,512,512]{2,1,0:T(8,128)S(1)}, u32[]{:S(2)}) copy-start(f32[1,512,512]{2,1,0:T(8,128)S(1)} %maximum_bitcast_fusion) | copy-start | bytes 3145732
  105.3 3.6 %copy-start.8 = (pred[512,512]{1,0:T(8,128)(4,1)S(1)}, pred[512,512]{1,0:T(8,128)(4,1)}, u32[]{:S(2)}) copy-start(pred[512,512]{1,0:T(8,128)(4,1)} %iota_compare_fusion) | copy-start | bytes 786436
  107.5 1.8 copy-start.3
  107.5 1.8 copy-start.5
  109.3 2.8 %slice-start.4 = ((f32[33,1024]{1,0:T(8,128)}), f32[32,1024]{1,0:T(8,128)S(1)}, s32[]{:S(2)}) async-start(f32[33,1024]{1,0:T(8,128)} %copy-done.6), calls=%async_computation.10 | async-start | bytes 262144 | tf_op jit(solution)/shard_map/slice | solution.py:150
  109.3 2.8 %copy-start.9 = (f32[32,2,512]{2,1,0:T(2,128)S(1)}, f32[32,2,512]{2,1,0:T(2,128)}, u32[]{:S(2)}) copy-start(f32[32,2,512]{2,1,0:T(2,128)} %slice.163) | copy-start | bytes 393220
  109.4 2.9 %copy-start.10 = (f32[2]{0:T(128)S(1)}, f32[2]{0:T(128)}, u32[]{:S(2)}) copy-start(f32[2]{0:T(128)} %constant.96.clone) | copy-start | bytes 28
  109.4 2.9 %copy-start.11 = (f32[2]{0:T(128)S(1)}, f32[2]{0:T(128)}, u32[]{:S(2)}) copy-start(f32[2]{0:T(128)} %constant.105) | copy-start | bytes 28
  112.4 17.7 %slice-start = ((s8[16777216]{0:T(1024)(128)(4,1)}), s8[4194304]{0:T(1024)(128)(4,1)S(1)}, s32[]{:S(2)}) async-start(s8[16777216]{0:T(1024)(128)(4,1)} %bitcast.190), calls=%async_computation.6 | async-start | bytes 8388608
  115.3 14.8 %slice-start.1 = ((s8[16777216]{0:T(1024)(128)(4,1)}), s8[4194304]{0:T(1024)(128)(4,1)S(1)}, s32[]{:S(2)}) async-start(s8[16777216]{0:T(1024)(128)(4,1)} %bitcast.190), calls=%async_computation.7 | async-start | bytes 8388608
  119.6 10.5 %slice-start.2 = ((s8[16777216]{0:T(1024)(128)(4,1)}), s8[4194304]{0:T(1024)(128)(4,1)S(1)}, s32[]{:S(2)}) async-start(s8[16777216]{0:T(1024)(128)(4,1)} %bitcast.190), calls=%async_computation.8 | async-start | bytes 8388608
  122.8 7.3 %slice-start.3 = ((s8[16777216]{0:T(1024)(128)(4,1)}), s8[4194304]{0:T(1024)(128)(4,1)S(1)}, s32[]{:S(2)}) async-start(s8[16777216]{0:T(1024)(128)(4,1)} %bitcast.190), calls=%async_computation.9 | async-start | bytes 8388608
  135.9 20.4 %all-to-all-start.5 = ((bf16[32,2,2,4096]{3,2,1,0:T(2,128)(2,1)}), bf16[32,2,2,4096]{3,2,1,0:T(2,128)(2,1)S(1)}, u32[]{:S(2)}, u32[]{:S(2)}) async-start(bf16[32,2,2,4096]{3,2,1,0:T(2,128)(2,1)} %copy.79), calls=%async_computation.5 | async-start | bytes 2097152 | tf_op jit(solution)/shard_map/all_to_all | solution.py:218
  156.3 19.4 %all-to-all-start.4 = ((bf16[32,2,2,4096]{3,2,1,0:T(2,128)(2,1)}), bf16[32,2,2,4096]{3,2,1,0:T(2,128)(2,1)S(1)}, u32[]{:S(2)}, u32[]{:S(2)}) async-start(bf16[32,2,2,4096]{3,2,1,0:T(2,128)(2,1)} %copy.77), calls=%async_computation.4 | async-start | bytes 2097152 | tf_op jit(solution)/shard_map/all_to_all | solution.py:218
  181.1 6.5 %collective-permute-start.1 = (f32[4,32,33]{2,1,0:T(8,128)S(1)}, f32[4,32,33]{2,1,0:T(8,128)S(1)}, u32[]{:S(2)}, u32[]{:S(2)}) collective-permute-start(f32[4,32,33]{2,1,0:T(8,128)S(1)} %pad_maximum_fusion.4), channel_id=1, source_target_pairs={{0,16},{8,24},{16,0},{24,8},{32,48},{40,56},{48,32},{56,40},{64,80... | collective-permute-start | bytes 50696 | tf_op jit(solution)/shard_map/ppermute | solution.py:79
  182.2 5.5 %collective-permute-start.2 = (f32[4,32,33]{2,1,0:T(8,128)S(1)}, f32[4,32,33]{2,1,0:T(8,128)S(1)}, u32[]{:S(2)}, u32[]{:S(2)}) collective-permute-start(f32[4,32,33]{2,1,0:T(8,128)S(1)} %pad_maximum_fusion.4), channel_id=1, source_target_pairs={{0,24},{8,0},{16,8},{24,16},{32,56},{40,32},{48,40},{56,48},{64,88... | collective-permute-start | bytes 50696 | tf_op jit(solution)/shard_map/ppermute | solution.py:79
  184.5 5.5 %collective-permute-start = (f32[4,32,33]{2,1,0:T(8,128)S(1)}, f32[4,32,33]{2,1,0:T(8,128)S(1)}, u32[]{:S(2)}, u32[]{:S(2)}) collective-permute-start(f32[4,32,33]{2,1,0:T(8,128)S(1)} %pad_maximum_fusion.4), channel_id=1, source_target_pairs={{0,8},{8,16},{16,24},{24,0},{32,40},{40,48},{48,56},{56,32},{64,72... | collective-permute-start | bytes 50696 | tf_op jit(solution)/shard_map/ppermute | solution.py:79
  190.0 4.3 %collective-permute-start.5 = (f32[4,32,33]{2,1,0:T(8,128)S(1)}, f32[4,32,33]{2,1,0:T(8,128)S(1)}, u32[]{:S(2)}, u32[]{:S(2)}) collective-permute-start(f32[4,32,33]{2,1,0:T(8,128)S(1)} %add_add_fusion.1), channel_id=1, source_target_pairs={{0,96},{8,104},{16,112},{24,120},{32,0},{40,8},{48,16},{56,24},{64... | collective-permute-start | bytes 50696 | tf_op jit(solution)/shard_map/ppermute | solution.py:79
  191.1 5.8 %collective-permute-start.4 = (f32[4,32,33]{2,1,0:T(8,128)S(1)}, f32[4,32,33]{2,1,0:T(8,128)S(1)}, u32[]{:S(2)}, u32[]{:S(2)}) collective-permute-start(f32[4,32,33]{2,1,0:T(8,128)S(1)} %add_add_fusion.1), channel_id=1, source_target_pairs={{0,64},{8,72},{16,80},{24,88},{32,96},{40,104},{48,112},{56,120},{... | collective-permute-start | bytes 50696 | tf_op jit(solution)/shard_map/ppermute | solution.py:79
  191.7 5.8 %collective-permute-start.3 = (f32[4,32,33]{2,1,0:T(8,128)S(1)}, f32[4,32,33]{2,1,0:T(8,128)S(1)}, u32[]{:S(2)}, u32[]{:S(2)}) collective-permute-start(f32[4,32,33]{2,1,0:T(8,128)S(1)} %add_add_fusion.1), channel_id=1, source_target_pairs={{0,32},{8,40},{16,48},{24,56},{32,64},{40,72},{48,80},{56,88},{64,... | collective-permute-start | bytes 50696 | tf_op jit(solution)/shard_map/ppermute | solution.py:79
where the time goes:
time: 216 us; the launch traced here: 213 us
  waiting for transfers between devices  67.8 us (31%)
  matrix products  52.2 us (24%)
  starting transfers between devices  46.9 us (22%)
  local copies, waits for them, and re-layouts  19.8 us (9%)
  other arithmetic  14.8 us (7%)
  Pallas kernels  10.5 us (5%)
    all_to_all x2, waiting for transfers between devices, per_device(): lax.all_to_all(feature, 'blk', split_axis=0, concat_axis=1, tiled=True)  26 us
    dot_general x2, matrix products, per_device(): jnp.einsum('si,sj->ij', xb, xb, preferred_element_type=jnp.float32)  19.9 us
    all_to_all x2, waiting for transfers between devices, exchange_sum(): lax.all_to_all(jnp.broadcast_to(chunk[None], (n,) + chunk.shape), axis, 0...  18.3 us
    all_to_all x2, starting transfers between devices, exchange_sum(): lax.all_to_all(jnp.broadcast_to(chunk[None], (n,) + chunk.shape), axis, 0...  17.8 us
    all_to_all x2, starting transfers between devices, exchange_sum(): pieces = lax.all_to_all(flat.reshape(n, -1, 128), axis, 0, 0, tiled=True)  15.2 us
    all_to_all x2, waiting for transfers between devices, exchange_sum(): pieces = lax.all_to_all(flat.reshape(n, -1, 128), axis, 0, 0, tiled=True)  13 us
    pallas_call x1, Pallas kernels, spd_solve(): pl.pallas_call(_spd_solve_kernel, out_shape=jax.ShapeDtypeStruct(b.shape,...  10.5 us
    ppermute x6, waiting for transfers between devices, butterfly_sum(): total = total + lax.ppermute(x, axis, perm)  10.5 us
  transfers between devices with their start and end apart: 12, of which 10 were waited for; matrix products, arithmetic and copies ran while one was open for 15% of the time, Pallas kernels for 0%

commit v1 on v0

--- a/solution.py
+++ b/solution.py
@@ -82,21 +82,30 @@
     return x
 
 
-def exchange_sum(arrays, axis):
+def scatter_sum(arrays, axis, wire):
     n = lax.axis_size(axis)
     flat = jnp.concatenate([a.reshape(-1) for a in arrays])
     size = flat.shape[0]
-    unit = n * 8 * 128
+    unit = n * 16 * 128
     flat = jnp.pad(flat, (0, -(-size // unit) * unit - size))
-    pieces = lax.all_to_all(flat.reshape(n, -1, 128), axis, 0, 0, tiled=True)
-    chunk = jnp.sum(pieces, axis=0)
-    whole = lax.all_to_all(jnp.broadcast_to(chunk[None], (n,) + chunk.shape), axis, 0, 0, tiled=True)
-    whole = whole.reshape(-1)
+    pieces = lax.all_to_all(flat.astype(wire).reshape(n, -1, 128), axis, 0, 0, tiled=True)
+    acc = jnp.int32 if jnp.issubdtype(wire, jnp.integer) else jnp.float32
+    return jnp.sum(pieces.astype(acc), axis=0).astype(jnp.float32), arrays
+
+
+def gather_split(parts, axis):
+    n = lax.axis_size(axis)
+    joined = jnp.concatenate([c for c, _ in parts], axis=0)
+    whole = lax.all_to_all(jnp.broadcast_to(joined[None], (n,) + joined.shape), axis, 0, 0, tiled=True)
     out = []
-    offset = 0
-    for a in arrays:
-        out.append(whole[offset:offset + a.size].reshape(a.shape))
-        offset += a.size
+    start = 0
+    for chunk, arrays in parts:
+        flat = whole[:, start:start + chunk.shape[0]].reshape(-1)
+        start += chunk.shape[0]
+        offset = 0
+        for a in arrays:
+            out.append(flat[offset:offset + a.size].reshape(a.shape))
+            offset += a.size
     return out
 
 
@@ -130,17 +139,24 @@
 
     gram_parts = []
     early_totals = []
+    gram_wire = jnp.uint16 if 4 * sample_rows <= 65535 else jnp.float32
     for b in range(block_count):
         xb = genotypes[:, b * B:(b + 1) * B]
         gram_parts.append(jnp.einsum("si,sj->ij", xb, xb, preferred_element_type=jnp.float32))
         if b + 1 < block_count:
-            early_totals += exchange_sum([pack(gram_parts[-1])], "fold")
+            early_totals += gather_split([scatter_sum([pack(gram_parts[-1])], "fold", gram_wire)], "fold")
     phen_aug = jnp.concatenate([phen, jnp.ones((1, sample_rows), phen.dtype)], axis=0)
     cross_aug = jnp.dot(phen_aug, genotypes, preferred_element_type=jnp.float32)
     phen_local = jnp.sum(phen.astype(jnp.float32), axis=1)
     phen_row = jnp.zeros((1, genotypes.shape[1]), jnp.float32).at[0, :p_size].set(phen_local)
     sums_local = jnp.concatenate([cross_aug, phen_row], axis=0)
-    totals = early_totals + exchange_sum([pack(gram_parts[-1]), sums_local], "fold")
+    totals = early_totals + gather_split(
+        [
+            scatter_sum([pack(gram_parts[-1])], "fold", gram_wire),
+            scatter_sum([sums_local], "fold", jnp.float32),
+        ],
+        "fold",
+    )
     sums_total = totals[-1]
     gram_part = jnp.stack(gram_parts)
     gram_sum = jnp.stack([unpack(p) for p in totals[:-1]])

time: 216 us -> 231 us (1.069)
  local copies, waits for them, and re-layouts: 19.8 us -> 26.1 us
  starting transfers between devices: 46.9 us -> 50.7 us
  waiting for transfers between devices: 67.8 us -> 70.4 us
    all_to_all x4 -> x5, starting transfers between devices: 33 us -> 36.7 us  [the longest x3 18.9 us: scatter_sum(): lax.all_to_all(flat.astype(wire).reshape(n, -1, 128), axis, 0, 0, tiled=T...]
    all_to_all x4 -> x5, waiting for transfers between devices: 31.3 us -> 33.8 us  [the longest x2 17.4 us: gather_split(): lax.all_to_all(jnp.broadcast_to(joined[None], (n,) + joined.shape), axis,...]
  transfers between devices with their start and end apart: 12 -> 13, of which waited for: 10 -> 11; matrix products, arithmetic and copies ran while one was open for 15% -> 15% of each run, Pallas kernels for 0% -> 0%
where the time goes in v1:
time: 231 us; the launch traced here: 228 us
  waiting for transfers between devices  70.4 us (30%)
  matrix products  52.2 us (23%)
  starting transfers between devices  50.7 us (22%)
  local copies, waits for them, and re-layouts  26.1 us (11%)
  other arithmetic  16.9 us (7%)
  Pallas kernels  10.5 us (5%)
    all_to_all x2, waiting for transfers between devices, per_device(): lax.all_to_all(feature, 'blk', split_axis=0, concat_axis=1, tiled=True)  26 us
    dot_general x2, matrix products, per_device(): jnp.einsum('si,sj->ij', xb, xb, preferred_element_type=jnp.float32)  19.9 us
    all_to_all x3, starting transfers between devices, scatter_sum(): lax.all_to_all(flat.astype(wire).reshape(n, -1, 128), axis, 0, 0, tiled=T...  18.9 us
    all_to_all x2, starting transfers between devices, gather_split(): lax.all_to_all(jnp.broadcast_to(joined[None], (n,) + joined.shape), axis,...  17.9 us
    all_to_all x2, waiting for transfers between devices, gather_split(): lax.all_to_all(jnp.broadcast_to(joined[None], (n,) + joined.shape), axis,...  17.4 us
    all_to_all x3, waiting for transfers between devices, scatter_sum(): lax.all_to_all(flat.astype(wire).reshape(n, -1, 128), axis, 0, 0, tiled=T...  16.4 us
    ppermute x6, waiting for transfers between devices, butterfly_sum(): total = total + lax.ppermute(x, axis, perm)  10.6 us
    pallas_call x1, Pallas kernels, spd_solve(): pl.pallas_call(_spd_solve_kernel, out_shape=jax.ShapeDtypeStruct(b.shape,...  10.5 us
  transfers between devices with their start and end apart: 13, of which 11 were waited for; matrix products, arithmetic and copies ran while one was open for 15% of the time, Pallas kernels for 0%

profile of v1, /device:TPU:0, one launch (start us, length us, event | category | flops | bytes accessed | tf_op | source)
XLA Modules:
  0.0 228.0 jit_solution(18345593020503373049)
XLA Ops:
  3.9 8.7 %fusion.91 = f32[33,1024]{1,0:T(8,128)S(1)} fusion(bf16[8192,1024]{1,0:T(8,128)(2,1)} %param.6, bf16[32,8192]{1,0:T(8,128)(2,1)S(1)} %get-tuple-element.20), kind=kOutput, calls=%fused_computation.71 | convolution fusion | flops 553648128 | bytes 17436672 | tf_op jit(solution)/shard_map/dot_general | solution.py:149
  13.4 8.0 %all-to-all-start.3 = ((f32[16,32,128]{2,1,0:T(8,128)}), f32[16,32,128]{2,1,0:T(8,128)S(1)}, u32[]{:S(2)}, u32[]{:S(2)}) async-start(f32[16,32,128]{2,1,0:T(8,128)} %bitcast.7), calls=%async_computation.3 | async-start | bytes 524288 | tf_op jit(solution)/shard_map/all_to_all | solution.py:91
  21.4 10.0 %fusion = f32[512,512]{1,0:T(8,128)S(1)} fusion(bf16[8192,1024]{1,0:T(8,128)(2,1)} %param.6), kind=kOutput, calls=%fused_computation.1 | convolution fusion | flops 4294967296 | bytes 9437184 | tf_op jit(solution)/shard_map/si,sj->ij/dot_general | solution.py:145
  31.4 9.9 %fusion.2 = f32[512,512]{1,0:T(8,128)S(1)} fusion(bf16[8192,1024]{1,0:T(8,128)(2,1)} %param.6), kind=kOutput, calls=%fused_computation.3 | convolution fusion | flops 4294967296 | bytes 9437184 | tf_op jit(solution)/shard_map/si,sj->ij/dot_general | solution.py:145
  43.4 7.2 %all-to-all-start = ((u16[16,80,128]{2,1,0:T(8,128)(2,1)}), u16[16,80,128]{2,1,0:T(8,128)(2,1)S(1)}, u32[]{:S(2)}, u32[]{:S(2)}) async-start(u16[16,80,128]{2,1,0:T(8,128)(2,1)} %bitcast), calls=%async_computation | async-start | bytes 655360 | tf_op jit(solution)/shard_map/all_to_all | solution.py:91
  51.8 7.7 %all-to-all-done = u16[16,80,128]{2,1,0:T(8,128)(2,1)S(1)} async-done(((u16[16,80,128]{2,1,0:T(8,128)(2,1)}), u16[16,80,128]{2,1,0:T(8,128)(2,1)S(1)}, u32[]{:S(2)}, u32[]{:S(2)}) %all-to-all-start) | async-done | bytes 327712 | tf_op jit(solution)/shard_map/all_to_all | solution.py:91
  59.5 3.7 %all-to-all-start.2 = ((u16[16,80,128]{2,1,0:T(8,128)(2,1)}), u16[16,80,128]{2,1,0:T(8,128)(2,1)S(1)}, u32[]{:S(2)}, u32[]{:S(2)}) async-start(u16[16,80,128]{2,1,0:T(8,128)(2,1)} %bitcast.5), calls=%async_computation.2 | async-start | bytes 655360 | tf_op jit(solution)/shard_map/all_to_all | solution.py:91
  63.3 8.7 %all-to-all-done.2 = u16[16,80,128]{2,1,0:T(8,128)(2,1)S(1)} async-done(((u16[16,80,128]{2,1,0:T(8,128)(2,1)}), u16[16,80,128]{2,1,0:T(8,128)(2,1)S(1)}, u32[]{:S(2)}, u32[]{:S(2)}) %all-to-all-start.2) | async-done | bytes 327712 | tf_op jit(solution)/shard_map/all_to_all | solution.py:91
  72.9 3.7 %all-to-all-start.1 = ((f32[16,80,128]{2,1,0:T(8,128)}), f32[16,80,128]{2,1,0:T(8,128)S(1)}, u32[]{:S(2)}, u32[]{:S(2)}) async-start(f32[16,80,128]{2,1,0:T(8,128)} %broadcast_in_dim.115), calls=%async_computation.1 | async-start | bytes 1310720 | tf_op jit(solution)/shard_map/all_to_all | solution.py:99
  76.7 10.7 %all-to-all-done.1 = f32[16,80,128]{2,1,0:T(8,128)S(1)} async-done(((f32[16,80,128]{2,1,0:T(8,128)}), f32[16,80,128]{2,1,0:T(8,128)S(1)}, u32[]{:S(2)}, u32[]{:S(2)}) %all-to-all-start.1) | async-done | bytes 655392 | tf_op jit(solution)/shard_map/all_to_all | solution.py:99
  88.4 14.2 %all-to-all-start.4 = ((f32[16,112,128]{2,1,0:T(8,128)}), f32[16,112,128]{2,1,0:T(8,128)S(1)}, u32[]{:S(2)}, u32[]{:S(2)}) async-start(f32[16,112,128]{2,1,0:T(8,128)} %broadcast_in_dim.121), calls=%async_computation.4 | async-start | bytes 1835008 | tf_op jit(solution)/shard_map/all_to_all | solution.py:99
  103.8 1.9 fusion.96
  107.7 6.8 %all-to-all-done.4 = f32[16,112,128]{2,1,0:T(8,128)S(1)} async-done(((f32[16,112,128]{2,1,0:T(8,128)}), f32[16,112,128]{2,1,0:T(8,128)S(1)}, u32[]{:S(2)}, u32[]{:S(2)}) %all-to-all-start.4) | async-done | bytes 917536 | tf_op jit(solution)/shard_map/all_to_all | solution.py:99
  124.1 2.6 %abs_reduce_fusion = (f32[2,512]{1,0:T(2,128)S(1)}, f32[2,512,512]{2,1,0:T(8,128)S(1)}) fusion(f32[2,512]{1,0:T(2,128)S(1)} %get-tuple-element.37, f32[2,512]{1,0:T(2,128)S(1)} %get-tuple-element.39, f32[2,512]{1,0:T(2,128)S(1)} %get-tuple-element.38, f32[2,512]{1,0:T(2,128)S(1)} %get-tuple-element.40, f32[1,512,512]{2,1,0:T(8,128)S(1)} %bitcast.195, ...), kind=kLoop, calls=%fused_computation.43 | loop fusion | flops 7339008 | bytes 6311936 | tf_op jit(solution)/shard_map/reduce_sum | solution.py:190
  130.0 1.5 multiply_add_fusion.2
  135.8 1.7 fusion.88
  137.5 3.7 %convolution_bitcast_fusion = f32[32,1,2,4096]{3,0,2,1:T(8,128)S(1)} fusion(bf16[8192,1024]{1,0:T(8,128)(2,1)} %param.6, bf16[2,2,32,512]{3,2,1,0:T(8,128)(2,1)S(1)} %fusion.88), kind=kOutput, calls=%fused_computation.5 | convolution fusion | flops 268435456 | bytes 5308416 | tf_op jit(solution)/shard_map/si,rpi->prs/dot_general | solution.py:223
  141.2 3.6 %convolution_bitcast_fusion.1 = f32[32,1,2,4096]{3,0,2,1:T(8,128)S(1)} fusion(bf16[8192,1024]{1,0:T(8,128)(2,1)} %param.6, bf16[2,2,32,512]{3,2,1,0:T(8,128)(2,1)S(1)} %fusion.88), kind=kOutput, calls=%fused_computation.6 | convolution fusion | flops 268435456 | bytes 5308416 | tf_op jit(solution)/shard_map/si,rpi->prs/dot_general | solution.py:223
  148.6 2.1 copy.79
  150.7 4.5 %all-to-all-start.6 = ((bf16[32,2,2,4096]{3,2,1,0:T(2,128)(2,1)}), bf16[32,2,2,4096]{3,2,1,0:T(2,128)(2,1)S(1)}, u32[]{:S(2)}, u32[]{:S(2)}) async-start(bf16[32,2,2,4096]{3,2,1,0:T(2,128)(2,1)} %copy.79), calls=%async_computation.6 | async-start | bytes 2097152 | tf_op jit(solution)/shard_map/all_to_all | solution.py:234
  155.2 2.1 copy.77
  157.2 13.9 %all-to-all-done.6 = bf16[32,2,2,4096]{3,2,1,0:T(2,128)(2,1)S(1)} async-done(((bf16[32,2,2,4096]{3,2,1,0:T(2,128)(2,1)}), bf16[32,2,2,4096]{3,2,1,0:T(2,128)(2,1)S(1)}, u32[]{:S(2)}, u32[]{:S(2)}) %all-to-all-start.6) | async-done | bytes 1048608 | tf_op jit(solution)/shard_map/all_to_all | solution.py:234
  171.1 3.6 %all-to-all-start.5 = ((bf16[32,2,2,4096]{3,2,1,0:T(2,128)(2,1)}), bf16[32,2,2,4096]{3,2,1,0:T(2,128)(2,1)S(1)}, u32[]{:S(2)}, u32[]{:S(2)}) async-start(bf16[32,2,2,4096]{3,2,1,0:T(2,128)(2,1)} %copy.77), calls=%async_computation.5 | async-start | bytes 2097152 | tf_op jit(solution)/shard_map/all_to_all | solution.py:234
  174.8 2.1 copy.108
  178.4 12.2 %all-to-all-done.5 = bf16[32,2,2,4096]{3,2,1,0:T(2,128)(2,1)S(1)} async-done(((bf16[32,2,2,4096]{3,2,1,0:T(2,128)(2,1)}), bf16[32,2,2,4096]{3,2,1,0:T(2,128)(2,1)S(1)}, u32[]{:S(2)}, u32[]{:S(2)}) %all-to-all-start.5) | async-done | bytes 1048608 | tf_op jit(solution)/shard_map/all_to_all | solution.py:234
  190.5 2.1 copy.109
  196.9 2.3 collective-permute-start.2
  199.2 3.2 %collective-permute-done.1 = f32[4,32,33]{2,1,0:T(8,128)S(1)} collective-permute-done((f32[4,32,33]{2,1,0:T(8,128)S(1)}, f32[4,32,33]{2,1,0:T(8,128)S(1)}, u32[]{:S(2)}, u32[]{:S(2)}) %collective-permute-start.1) | collective-permute-done | bytes 16928 | tf_op jit(solution)/shard_map/ppermute | solution.py:79
  202.4 2.3 %collective-permute-done = f32[4,32,33]{2,1,0:T(8,128)S(1)} collective-permute-done((f32[4,32,33]{2,1,0:T(8,128)S(1)}, f32[4,32,33]{2,1,0:T(8,128)S(1)}, u32[]{:S(2)}, u32[]{:S(2)}) %collective-permute-start) | collective-permute-done | bytes 16928 | tf_op jit(solution)/shard_map/ppermute | solution.py:79
  207.3 1.8 collective-permute-done.5
  209.1 2.7 %collective-permute-done.4 = f32[4,32,33]{2,1,0:T(8,128)S(1)} collective-permute-done((f32[4,32,33]{2,1,0:T(8,128)S(1)}, f32[4,32,33]{2,1,0:T(8,128)S(1)}, u32[]{:S(2)}, u32[]{:S(2)}) %collective-permute-start.4) | collective-permute-done | bytes 16928 | tf_op jit(solution)/shard_map/ppermute | solution.py:79
  214.2 10.5 %shard_map.46 = f32[4,32,1]{2,1,0:T(8,128)} custom-call(f32[4,32,32]{2,1,0:T(8,128)} %multiply_add_fusion.11.a_ref, f32[4,32,1]{2,1,0:T(8,128)} %copy.82.b_ref), custom_call_target="tpu_custom_call" | custom-call | tf_op jit(solution)/shard_map/pallas_call | solution.py:60
  (137 shorter events, 47.6 us)
Async XLA Ops:
  0.0 2.0 copy-start
  12.6 90.0 %copy-start.6 = (f32[33,1024]{1,0:T(8,128)}, f32[33,1024]{1,0:T(8,128)S(1)}, u32[]{:S(2)}) copy-start(f32[33,1024]{1,0:T(8,128)S(1)} %fusion.91) | copy-start | bytes 405508
  13.4 30.0 %all-to-all-start.3 = ((f32[16,32,128]{2,1,0:T(8,128)}), f32[16,32,128]{2,1,0:T(8,128)S(1)}, u32[]{:S(2)}, u32[]{:S(2)}) async-start(f32[16,32,128]{2,1,0:T(8,128)} %bitcast.7), calls=%async_computation.3 | async-start | bytes 524288 | tf_op jit(solution)/shard_map/all_to_all | solution.py:91
  31.4 19.3 %copy-start.2 = (f32[512,512]{1,0:T(8,128)}, f32[512,512]{1,0:T(8,128)S(1)}, u32[]{:S(2)}) copy-start(f32[512,512]{1,0:T(8,128)S(1)} %fusion) | copy-start | bytes 3145732
  41.3 1.0 copy-start.4
  43.4 7.4 %copy-start.7 = (f32[16,32,128]{2,1,0:T(8,128)}, f32[16,32,128]{2,1,0:T(8,128)S(1)}, u32[]{:S(2)}) copy-start(f32[16,32,128]{2,1,0:T(8,128)S(1)} %all-to-all-done.3) | copy-start | bytes 786436
  43.4 16.0 %all-to-all-start = ((u16[16,80,128]{2,1,0:T(8,128)(2,1)}), u16[16,80,128]{2,1,0:T(8,128)(2,1)S(1)}, u32[]{:S(2)}, u32[]{:S(2)}) async-start(u16[16,80,128]{2,1,0:T(8,128)(2,1)} %bitcast), calls=%async_computation | async-start | bytes 655360 | tf_op jit(solution)/shard_map/all_to_all | solution.py:91
  50.9 25.7 %copy-start.8 = (f32[16,32,128]{2,1,0:T(8,128)S(1)}, f32[16,32,128]{2,1,0:T(8,128)}, u32[]{:S(2)}) copy-start(f32[16,32,128]{2,1,0:T(8,128)} %copy-done.7) | copy-start | bytes 786436
  59.5 12.5 %all-to-all-start.2 = ((u16[16,80,128]{2,1,0:T(8,128)(2,1)}), u16[16,80,128]{2,1,0:T(8,128)(2,1)S(1)}, u32[]{:S(2)}, u32[]{:S(2)}) async-start(u16[16,80,128]{2,1,0:T(8,128)(2,1)} %bitcast.5), calls=%async_computation.2 | async-start | bytes 655360 | tf_op jit(solution)/shard_map/all_to_all | solution.py:91
  72.9 14.5 %all-to-all-start.1 = ((f32[16,80,128]{2,1,0:T(8,128)}), f32[16,80,128]{2,1,0:T(8,128)S(1)}, u32[]{:S(2)}, u32[]{:S(2)}) async-start(f32[16,80,128]{2,1,0:T(8,128)} %broadcast_in_dim.115), calls=%async_computation.1 | async-start | bytes 1310720 | tf_op jit(solution)/shard_map/all_to_all | solution.py:99
  88.4 26.1 %all-to-all-start.4 = ((f32[16,112,128]{2,1,0:T(8,128)}), f32[16,112,128]{2,1,0:T(8,128)S(1)}, u32[]{:S(2)}, u32[]{:S(2)}) async-start(f32[16,112,128]{2,1,0:T(8,128)} %broadcast_in_dim.121), calls=%async_computation.4 | async-start | bytes 1835008 | tf_op jit(solution)/shard_map/all_to_all | solution.py:99
  107.7 15.2 %copy-start.1 = (f32[1,512,512]{2,1,0:T(8,128)}, f32[1,512,512]{2,1,0:T(8,128)S(1)}, u32[]{:S(2)}) copy-start(f32[1,512,512]{2,1,0:T(8,128)S(1)} %maximum_bitcast_fusion) | copy-start | bytes 3145732
  121.5 2.5 %copy-start.3 = (f32[512,512]{1,0:T(8,128)S(1)}, f32[512,512]{1,0:T(8,128)}, u32[]{:S(2)}) copy-start(f32[512,512]{1,0:T(8,128)} %copy-done.2) | copy-start | bytes 3145732
  121.5 2.5 %copy-start.5 = (f32[512,512]{1,0:T(8,128)S(1)}, f32[512,512]{1,0:T(8,128)}, u32[]{:S(2)}) copy-start(f32[512,512]{1,0:T(8,128)} %copy-done.4) | copy-start | bytes 3145732
  124.1 2.8 %slice-start.4 = ((f32[33,1024]{1,0:T(8,128)}), f32[32,1024]{1,0:T(8,128)S(1)}, s32[]{:S(2)}) async-start(f32[33,1024]{1,0:T(8,128)} %copy-done.6), calls=%async_computation.11 | async-start | bytes 262144 | tf_op jit(solution)/shard_map/slice | solution.py:166
  124.1 2.8 %copy-start.9 = (f32[32,2,512]{2,1,0:T(2,128)S(1)}, f32[32,2,512]{2,1,0:T(2,128)}, u32[]{:S(2)}) copy-start(f32[32,2,512]{2,1,0:T(2,128)} %slice.181) | copy-start | bytes 393220
  124.1 2.9 %copy-start.10 = (f32[2]{0:T(128)S(1)}, f32[2]{0:T(128)}, u32[]{:S(2)}) copy-start(f32[2]{0:T(128)} %constant.98.clone) | copy-start | bytes 28
  124.1 2.9 %copy-start.11 = (f32[2]{0:T(128)S(1)}, f32[2]{0:T(128)}, u32[]{:S(2)}) copy-start(f32[2]{0:T(128)} %constant.109) | copy-start | bytes 28
  127.1 17.7 %slice-start = ((s8[16777216]{0:T(1024)(128)(4,1)}), s8[4194304]{0:T(1024)(128)(4,1)S(1)}, s32[]{:S(2)}) async-start(s8[16777216]{0:T(1024)(128)(4,1)} %bitcast.189), calls=%async_computation.7 | async-start | bytes 8388608
  130.0 14.8 %slice-start.1 = ((s8[16777216]{0:T(1024)(128)(4,1)}), s8[4194304]{0:T(1024)(128)(4,1)S(1)}, s32[]{:S(2)}) async-start(s8[16777216]{0:T(1024)(128)(4,1)} %bitcast.189), calls=%async_computation.8 | async-start | bytes 8388608
  134.4 10.5 %slice-start.2 = ((s8[16777216]{0:T(1024)(128)(4,1)}), s8[4194304]{0:T(1024)(128)(4,1)S(1)}, s32[]{:S(2)}) async-start(s8[16777216]{0:T(1024)(128)(4,1)} %bitcast.189), calls=%async_computation.9 | async-start | bytes 8388608
  137.5 7.3 %slice-start.3 = ((s8[16777216]{0:T(1024)(128)(4,1)}), s8[4194304]{0:T(1024)(128)(4,1)S(1)}, s32[]{:S(2)}) async-start(s8[16777216]{0:T(1024)(128)(4,1)} %bitcast.189), calls=%async_computation.10 | async-start | bytes 8388608
  150.7 20.4 %all-to-all-start.6 = ((bf16[32,2,2,4096]{3,2,1,0:T(2,128)(2,1)}), bf16[32,2,2,4096]{3,2,1,0:T(2,128)(2,1)S(1)}, u32[]{:S(2)}, u32[]{:S(2)}) async-start(bf16[32,2,2,4096]{3,2,1,0:T(2,128)(2,1)} %copy.79), calls=%async_computation.6 | async-start | bytes 2097152 | tf_op jit(solution)/shard_map/all_to_all | solution.py:234
  171.1 19.4 %all-to-all-start.5 = ((bf16[32,2,2,4096]{3,2,1,0:T(2,128)(2,1)}), bf16[32,2,2,4096]{3,2,1,0:T(2,128)(2,1)S(1)}, u32[]{:S(2)}, u32[]{:S(2)}) async-start(bf16[32,2,2,4096]{3,2,1,0:T(2,128)(2,1)} %copy.77), calls=%async_computation.5 | async-start | bytes 2097152 | tf_op jit(solution)/shard_map/all_to_all | solution.py:234
  195.9 6.5 %collective-permute-start.1 = (f32[4,32,33]{2,1,0:T(8,128)S(1)}, f32[4,32,33]{2,1,0:T(8,128)S(1)}, u32[]{:S(2)}, u32[]{:S(2)}) collective-permute-start(f32[4,32,33]{2,1,0:T(8,128)S(1)} %pad_maximum_fusion.2), channel_id=1, source_target_pairs={{0,16},{8,24},{16,0},{24,8},{32,48},{40,56},{48,32},{56,40},{64,80... | collective-permute-start | bytes 50696 | tf_op jit(solution)/shard_map/ppermute | solution.py:79
  196.9 5.5 %collective-permute-start.2 = (f32[4,32,33]{2,1,0:T(8,128)S(1)}, f32[4,32,33]{2,1,0:T(8,128)S(1)}, u32[]{:S(2)}, u32[]{:S(2)}) collective-permute-start(f32[4,32,33]{2,1,0:T(8,128)S(1)} %pad_maximum_fusion.2), channel_id=1, source_target_pairs={{0,24},{8,0},{16,8},{24,16},{32,56},{40,32},{48,40},{56,48},{64,88... | collective-permute-start | bytes 50696 | tf_op jit(solution)/shard_map/ppermute | solution.py:79
  199.2 5.5 %collective-permute-start = (f32[4,32,33]{2,1,0:T(8,128)S(1)}, f32[4,32,33]{2,1,0:T(8,128)S(1)}, u32[]{:S(2)}, u32[]{:S(2)}) collective-permute-start(f32[4,32,33]{2,1,0:T(8,128)S(1)} %pad_maximum_fusion.2), channel_id=1, source_target_pairs={{0,8},{8,16},{16,24},{24,0},{32,40},{40,48},{48,56},{56,32},{64,72... | collective-permute-start | bytes 50696 | tf_op jit(solution)/shard_map/ppermute | solution.py:79
  204.8 4.3 %collective-permute-start.5 = (f32[4,32,33]{2,1,0:T(8,128)S(1)}, f32[4,32,33]{2,1,0:T(8,128)S(1)}, u32[]{:S(2)}, u32[]{:S(2)}) collective-permute-start(f32[4,32,33]{2,1,0:T(8,128)S(1)} %add_add_fusion.1), channel_id=1, source_target_pairs={{0,96},{8,104},{16,112},{24,120},{32,0},{40,8},{48,16},{56,24},{64... | collective-permute-start | bytes 50696 | tf_op jit(solution)/shard_map/ppermute | solution.py:79
  206.0 5.8 %collective-permute-start.4 = (f32[4,32,33]{2,1,0:T(8,128)S(1)}, f32[4,32,33]{2,1,0:T(8,128)S(1)}, u32[]{:S(2)}, u32[]{:S(2)}) collective-permute-start(f32[4,32,33]{2,1,0:T(8,128)S(1)} %add_add_fusion.1), channel_id=1, source_target_pairs={{0,64},{8,72},{16,80},{24,88},{32,96},{40,104},{48,112},{56,120},{... | collective-permute-start | bytes 50696 | tf_op jit(solution)/shard_map/ppermute | solution.py:79
  206.5 5.9 %collective-permute-start.3 = (f32[4,32,33]{2,1,0:T(8,128)S(1)}, f32[4,32,33]{2,1,0:T(8,128)S(1)}, u32[]{:S(2)}, u32[]{:S(2)}) collective-permute-start(f32[4,32,33]{2,1,0:T(8,128)S(1)} %add_add_fusion.1), channel_id=1, source_target_pairs={{0,32},{8,40},{16,48},{24,56},{32,64},{40,72},{48,80},{56,88},{64,... | collective-permute-start | bytes 50696 | tf_op jit(solution)/shard_map/ppermute | solution.py:79

commit v2 on v0

--- a/solution.py
+++ b/solution.py
@@ -182,7 +182,7 @@
                 "brpi,bij->brpj",
                 direction,
                 system,
-                precision=lax.Precision.HIGHEST,
+                precision=lax.Precision.HIGH,
                 preferred_element_type=jnp.float32,
             )
             + low_edge * direction

time: 216 us -> 199 us (0.921)
  starting transfers between devices: 46.9 us -> 36.6 us
  matrix products: 52.2 us -> 47.6 us
    all_to_all x2, starting transfers between devices: 17.8 us -> 7.5 us  [exchange_sum(): lax.all_to_all(jnp.broadcast_to(chunk[None], (n,) + chunk.shape), axis, 0...]
    dot_general x7, matrix products: 10.3 us -> 5.89 us  [times_system(): jnp.einsum('brpi,bij->brpj', direction, system, precision=lax.Precision.H...]
  transfers between devices with their start and end apart: 12 -> 12, of which waited for: 10 -> 10; matrix products, arithmetic and copies ran while one was open for 15% -> 16% of each run, Pallas kernels for 0% -> 0%
where the time goes in v2:
time: 199 us; the launch traced here: 198 us
  waiting for transfers between devices  67.8 us (34%)
  matrix products  47.6 us (24%)
  starting transfers between devices  36.6 us (18%)
  local copies, waits for them, and re-layouts  19.8 us (10%)
  other arithmetic  14.8 us (7%)
  Pallas kernels  10.5 us (5%)
    all_to_all x2, waiting for transfers between devices, per_device(): lax.all_to_all(feature, 'blk', split_axis=0, concat_axis=1, tiled=True)  25.8 us
    dot_general x2, matrix products, per_device(): jnp.einsum('si,sj->ij', xb, xb, preferred_element_type=jnp.float32)  19.9 us
    all_to_all x2, waiting for transfers between devices, exchange_sum(): lax.all_to_all(jnp.broadcast_to(chunk[None], (n,) + chunk.shape), axis, 0...  18.3 us
    all_to_all x2, starting transfers between devices, exchange_sum(): pieces = lax.all_to_all(flat.reshape(n, -1, 128), axis, 0, 0, tiled=True)  15.2 us
    all_to_all x2, waiting for transfers between devices, exchange_sum(): pieces = lax.all_to_all(flat.reshape(n, -1, 128), axis, 0, 0, tiled=True)  13 us
    ppermute x6, waiting for transfers between devices, butterfly_sum(): total = total + lax.ppermute(x, axis, perm)  10.7 us
    pallas_call x1, Pallas kernels, spd_solve(): pl.pallas_call(_spd_solve_kernel, out_shape=jax.ShapeDtypeStruct(b.shape,...  10.5 us
    dot_general x4, matrix products, per_device(): jnp.einsum('si,rpi->prs', genotypes[rows_h, b * B:(b + 1) * B], scaled[b]...  10.1 us
  transfers between devices with their start and end apart: 12, of which 10 were waited for; matrix products, arithmetic and copies ran while one was open for 16% of the time, Pallas kernels for 0%

profile of v2, /device:TPU:0, one launch (start us, length us, event | category | flops | bytes accessed | tf_op | source)
XLA Modules:
  0.0 197.8 jit_solution(11525908696873625509)
XLA Ops:
  0.0 9.9 %fusion.2 = f32[512,512]{1,0:T(8,128)S(1)} fusion(bf16[8192,1024]{1,0:T(8,128)(2,1)} %param.6), kind=kOutput, calls=%fused_computation.3 | convolution fusion | flops 4294967296 | bytes 9437184 | tf_op jit(solution)/shard_map/si,sj->ij/dot_general | solution.py:135
  12.0 8.0 %all-to-all-start = ((f32[16,72,128]{2,1,0:T(8,128)}), f32[16,72,128]{2,1,0:T(8,128)S(1)}, u32[]{:S(2)}, u32[]{:S(2)}) async-start(f32[16,72,128]{2,1,0:T(8,128)} %bitcast.1), calls=%async_computation | async-start | bytes 1179648 | tf_op jit(solution)/shard_map/all_to_all | solution.py:91
  20.6 10.0 %fusion = f32[512,512]{1,0:T(8,128)S(1)} fusion(bf16[8192,1024]{1,0:T(8,128)(2,1)} %param.6), kind=kOutput, calls=%fused_computation.1 | convolution fusion | flops 4294967296 | bytes 9437184 | tf_op jit(solution)/shard_map/si,sj->ij/dot_general | solution.py:135
  31.9 8.7 %fusion.91 = f32[33,1024]{1,0:T(8,128)S(1)} fusion(bf16[8192,1024]{1,0:T(8,128)(2,1)} %param.6, bf16[32,8192]{1,0:T(8,128)(2,1)S(1)} %get-tuple-element.20), kind=kOutput, calls=%fused_computation.73 | convolution fusion | flops 553648128 | bytes 17436672 | tf_op jit(solution)/shard_map/dot_general | solution.py:139
  42.5 7.2 %all-to-all-start.2 = ((f32[16,88,128]{2,1,0:T(8,128)}), f32[16,88,128]{2,1,0:T(8,128)S(1)}, u32[]{:S(2)}, u32[]{:S(2)}) async-start(f32[16,88,128]{2,1,0:T(8,128)} %bitcast.8), calls=%async_computation.2 | async-start | bytes 1441792 | tf_op jit(solution)/shard_map/all_to_all | solution.py:91
  49.8 13.0 %all-to-all-done.2 = f32[16,88,128]{2,1,0:T(8,128)S(1)} async-done(((f32[16,88,128]{2,1,0:T(8,128)}), f32[16,88,128]{2,1,0:T(8,128)S(1)}, u32[]{:S(2)}, u32[]{:S(2)}) %all-to-all-start.2) | async-done | bytes 720928 | tf_op jit(solution)/shard_map/all_to_all | solution.py:91
  63.7 3.7 %all-to-all-start.1 = ((f32[16,72,128]{2,1,0:T(8,128)}), f32[16,72,128]{2,1,0:T(8,128)S(1)}, u32[]{:S(2)}, u32[]{:S(2)}) async-start(f32[16,72,128]{2,1,0:T(8,128)} %broadcast_in_dim.113), calls=%async_computation.1 | async-start | bytes 1179648 | tf_op jit(solution)/shard_map/all_to_all | solution.py:93
  67.4 10.8 %all-to-all-done.1 = f32[16,72,128]{2,1,0:T(8,128)S(1)} async-done(((f32[16,72,128]{2,1,0:T(8,128)}), f32[16,72,128]{2,1,0:T(8,128)S(1)}, u32[]{:S(2)}, u32[]{:S(2)}) %all-to-all-start.1) | async-done | bytes 589856 | tf_op jit(solution)/shard_map/all_to_all | solution.py:93
  79.1 3.8 %all-to-all-start.3 = ((f32[16,88,128]{2,1,0:T(8,128)}), f32[16,88,128]{2,1,0:T(8,128)S(1)}, u32[]{:S(2)}, u32[]{:S(2)}) async-start(f32[16,88,128]{2,1,0:T(8,128)} %broadcast_in_dim.119), calls=%async_computation.3 | async-start | bytes 1441792 | tf_op jit(solution)/shard_map/all_to_all | solution.py:93
  86.3 7.6 %all-to-all-done.3 = f32[16,88,128]{2,1,0:T(8,128)S(1)} async-done(((f32[16,88,128]{2,1,0:T(8,128)}), f32[16,88,128]{2,1,0:T(8,128)S(1)}, u32[]{:S(2)}, u32[]{:S(2)}) %all-to-all-start.3) | async-done | bytes 720928 | tf_op jit(solution)/shard_map/all_to_all | solution.py:93
  97.3 1.3 maximum_bitcast_fusion.1
  99.1 2.6 %abs_reduce_fusion = (f32[2,512]{1,0:T(2,128)S(1)}, f32[2,512,512]{2,1,0:T(8,128)S(1)}) fusion(f32[2,512]{1,0:T(2,128)S(1)} %get-tuple-element.37, f32[2,512]{1,0:T(2,128)S(1)} %get-tuple-element.38, f32[2,512]{1,0:T(2,128)S(1)} %get-tuple-element.39, f32[2,512]{1,0:T(2,128)S(1)} %get-tuple-element.40, f32[1,512,512]{2,1,0:T(8,128)S(1)} %bitcast.201, ...), kind=kLoop, calls=%fused_computation.43 | loop fusion | flops 7339008 | bytes 6311936 | tf_op jit(solution)/shard_map/reduce_sum | solution.py:174
  108.2 3.7 %convolution_bitcast_fusion = f32[32,1,2,4096]{3,0,2,1:T(8,128)S(1)} fusion(bf16[8192,1024]{1,0:T(8,128)(2,1)} %param.6, bf16[2,2,32,512]{3,2,1,0:T(8,128)(2,1)S(1)} %fusion.88), kind=kOutput, calls=%fused_computation.5 | convolution fusion | flops 268435456 | bytes 5308416 | tf_op jit(solution)/shard_map/si,rpi->prs/dot_general | solution.py:207
  111.9 3.6 %convolution_bitcast_fusion.1 = f32[32,1,2,4096]{3,0,2,1:T(8,128)S(1)} fusion(bf16[8192,1024]{1,0:T(8,128)(2,1)} %param.6, bf16[2,2,32,512]{3,2,1,0:T(8,128)(2,1)S(1)} %fusion.88), kind=kOutput, calls=%fused_computation.6 | convolution fusion | flops 268435456 | bytes 5308416 | tf_op jit(solution)/shard_map/si,rpi->prs/dot_general | solution.py:207
  115.5 1.4 convolution_bitcast_fusion.2
  116.9 1.4 convolution_bitcast_fusion.3
  119.0 2.1 %copy.79 = bf16[32,2,2,4096]{3,2,1,0:T(2,128)(2,1)} copy(bf16[32,2,2,4096]{3,0,2,1:T(8,128)(2,1)S(1)} %get-tuple-element.41) | data formatting | bytes 2097152 | tf_op jit(solution)/shard_map/convert_element_type | solution.py:217
  121.1 4.5 %all-to-all-start.5 = ((bf16[32,2,2,4096]{3,2,1,0:T(2,128)(2,1)}), bf16[32,2,2,4096]{3,2,1,0:T(2,128)(2,1)S(1)}, u32[]{:S(2)}, u32[]{:S(2)}) async-start(bf16[32,2,2,4096]{3,2,1,0:T(2,128)(2,1)} %copy.79), calls=%async_computation.5 | async-start | bytes 2097152 | tf_op jit(solution)/shard_map/all_to_all | solution.py:218
  125.6 2.1 %copy.77 = bf16[32,2,2,4096]{3,2,1,0:T(2,128)(2,1)} copy(bf16[32,2,2,4096]{3,0,2,1:T(8,128)(2,1)S(1)} %get-tuple-element.42) | data formatting | bytes 2097152 | tf_op jit(solution)/shard_map/convert_element_type | solution.py:217
  127.7 13.9 %all-to-all-done.5 = bf16[32,2,2,4096]{3,2,1,0:T(2,128)(2,1)S(1)} async-done(((bf16[32,2,2,4096]{3,2,1,0:T(2,128)(2,1)}), bf16[32,2,2,4096]{3,2,1,0:T(2,128)(2,1)S(1)}, u32[]{:S(2)}, u32[]{:S(2)}) %all-to-all-start.5) | async-done | bytes 1048608 | tf_op jit(solution)/shard_map/all_to_all | solution.py:218
  141.5 3.8 %all-to-all-start.4 = ((bf16[32,2,2,4096]{3,2,1,0:T(2,128)(2,1)}), bf16[32,2,2,4096]{3,2,1,0:T(2,128)(2,1)S(1)}, u32[]{:S(2)}, u32[]{:S(2)}) async-start(bf16[32,2,2,4096]{3,2,1,0:T(2,128)(2,1)} %copy.77), calls=%async_computation.4 | async-start | bytes 2097152 | tf_op jit(solution)/shard_map/all_to_all | solution.py:218
  145.4 2.1 %copy.108 = bf16[8,4,2,2,4096]{4,3,2,0,1:T(2,128)(2,1)} copy(bf16[8,4,2,2,4096]{4,3,2,1,0:T(2,128)(2,1)S(1)} %bitcast.192) | data formatting | bytes 2097152 | tf_op jit(solution)/shard_map/all_to_all | solution.py:218
  147.5 1.5 reshape.899
  149.0 11.9 %all-to-all-done.4 = bf16[32,2,2,4096]{3,2,1,0:T(2,128)(2,1)S(1)} async-done(((bf16[32,2,2,4096]{3,2,1,0:T(2,128)(2,1)}), bf16[32,2,2,4096]{3,2,1,0:T(2,128)(2,1)S(1)}, u32[]{:S(2)}, u32[]{:S(2)}) %all-to-all-start.4) | async-done | bytes 1048608 | tf_op jit(solution)/shard_map/all_to_all | solution.py:218
  161.0 2.1 %copy.109 = bf16[8,4,2,2,4096]{4,3,2,0,1:T(2,128)(2,1)} copy(bf16[8,4,2,2,4096]{4,3,2,1,0:T(2,128)(2,1)S(1)} %bitcast.193) | data formatting | bytes 2097152 | tf_op jit(solution)/shard_map/all_to_all | solution.py:218
  163.1 1.5 reshape.898
  167.4 2.3 %collective-permute-start.2 = (f32[4,32,33]{2,1,0:T(8,128)S(1)}, f32[4,32,33]{2,1,0:T(8,128)S(1)}, u32[]{:S(2)}, u32[]{:S(2)}) collective-permute-start(f32[4,32,33]{2,1,0:T(8,128)S(1)} %pad_maximum_fusion.4), channel_id=1, source_target_pairs={{0,24},{8,0},{16,8},{24,16},{32,56},{40,32},{48,40},{56,48},{64,88... | collective-permute-start | bytes 50696 | tf_op jit(solution)/shard_map/ppermute | solution.py:79
  169.7 3.2 %collective-permute-done.1 = f32[4,32,33]{2,1,0:T(8,128)S(1)} collective-permute-done((f32[4,32,33]{2,1,0:T(8,128)S(1)}, f32[4,32,33]{2,1,0:T(8,128)S(1)}, u32[]{:S(2)}, u32[]{:S(2)}) %collective-permute-start.1) | collective-permute-done | bytes 16928 | tf_op jit(solution)/shard_map/ppermute | solution.py:79
  172.9 2.3 %collective-permute-done = f32[4,32,33]{2,1,0:T(8,128)S(1)} collective-permute-done((f32[4,32,33]{2,1,0:T(8,128)S(1)}, f32[4,32,33]{2,1,0:T(8,128)S(1)}, u32[]{:S(2)}, u32[]{:S(2)}) %collective-permute-start) | collective-permute-done | bytes 16928 | tf_op jit(solution)/shard_map/ppermute | solution.py:79
  177.5 2.0 %collective-permute-done.5 = f32[4,32,33]{2,1,0:T(8,128)S(1)} collective-permute-done((f32[4,32,33]{2,1,0:T(8,128)S(1)}, f32[4,32,33]{2,1,0:T(8,128)S(1)}, u32[]{:S(2)}, u32[]{:S(2)}) %collective-permute-start.5) | collective-permute-done | bytes 16928 | tf_op jit(solution)/shard_map/ppermute | solution.py:79
  179.6 2.5 %collective-permute-done.4 = f32[4,32,33]{2,1,0:T(8,128)S(1)} collective-permute-done((f32[4,32,33]{2,1,0:T(8,128)S(1)}, f32[4,32,33]{2,1,0:T(8,128)S(1)}, u32[]{:S(2)}, u32[]{:S(2)}) %collective-permute-start.4) | collective-permute-done | bytes 16928 | tf_op jit(solution)/shard_map/ppermute | solution.py:79
  184.5 10.5 %shard_map.46 = f32[4,32,1]{2,1,0:T(8,128)} custom-call(f32[4,32,32]{2,1,0:T(8,128)} %multiply_add_fusion.11.a_ref, f32[4,32,1]{2,1,0:T(8,128)} %copy.82.b_ref), custom_call_target="tpu_custom_call" | custom-call | tf_op jit(solution)/shard_map/pallas_call | solution.py:60
  (128 shorter events, 32.2 us)
Async XLA Ops:
  0.0 30.7 %copy-start = (bf16[32,8192]{1,0:T(8,128)(2,1)S(1)}, bf16[32,8192]{1,0:T(8,128)(2,1)}, u32[]{:S(2)}) copy-start(bf16[32,8192]{1,0:T(8,128)(2,1)} %param.7) | copy-start | bytes 1572868
  9.9 1.0 copy-start.2
  11.0 9.6 %copy-start.12 = (s32[32]{0:T(128)S(1)}, s32[32]{0:T(128)}, u32[]{:S(2)}) copy-start(s32[32]{0:T(128)} %param.8) | copy-start | bytes 388
  12.0 30.6 %all-to-all-start = ((f32[16,72,128]{2,1,0:T(8,128)}), f32[16,72,128]{2,1,0:T(8,128)S(1)}, u32[]{:S(2)}, u32[]{:S(2)}) async-start(f32[16,72,128]{2,1,0:T(8,128)} %bitcast.1), calls=%async_computation | async-start | bytes 1179648 | tf_op jit(solution)/shard_map/all_to_all | solution.py:91
  30.6 10.8 %copy-start.4 = (f32[512,512]{1,0:T(8,128)}, f32[512,512]{1,0:T(8,128)S(1)}, u32[]{:S(2)}) copy-start(f32[512,512]{1,0:T(8,128)S(1)} %fusion) | copy-start | bytes 3145732
  40.6 0.7 copy-start.6
  42.5 20.3 %all-to-all-start.2 = ((f32[16,88,128]{2,1,0:T(8,128)}), f32[16,88,128]{2,1,0:T(8,128)S(1)}, u32[]{:S(2)}, u32[]{:S(2)}) async-start(f32[16,88,128]{2,1,0:T(8,128)} %bitcast.8), calls=%async_computation.2 | async-start | bytes 1441792 | tf_op jit(solution)/shard_map/all_to_all | solution.py:91
  63.7 19.3 %copy-start.7 = (f32[33,1024]{1,0:T(8,128)S(1)}, f32[33,1024]{1,0:T(8,128)}, u32[]{:S(2)}) copy-start(f32[33,1024]{1,0:T(8,128)} %copy-done.6) | copy-start | bytes 405508
  63.7 14.5 %all-to-all-start.1 = ((f32[16,72,128]{2,1,0:T(8,128)}), f32[16,72,128]{2,1,0:T(8,128)S(1)}, u32[]{:S(2)}, u32[]{:S(2)}) async-start(f32[16,72,128]{2,1,0:T(8,128)} %broadcast_in_dim.113), calls=%async_computation.1 | async-start | bytes 1179648 | tf_op jit(solution)/shard_map/all_to_all | solution.py:93
  79.1 14.8 %all-to-all-start.3 = ((f32[16,88,128]{2,1,0:T(8,128)}), f32[16,88,128]{2,1,0:T(8,128)S(1)}, u32[]{:S(2)}, u32[]{:S(2)}) async-start(f32[16,88,128]{2,1,0:T(8,128)} %broadcast_in_dim.119), calls=%async_computation.3 | async-start | bytes 1441792 | tf_op jit(solution)/shard_map/all_to_all | solution.py:93
  86.3 12.3 %copy-start.1 = (f32[1,512,512]{2,1,0:T(8,128)}, f32[1,512,512]{2,1,0:T(8,128)S(1)}, u32[]{:S(2)}) copy-start(f32[1,512,512]{2,1,0:T(8,128)S(1)} %maximum_bitcast_fusion) | copy-start | bytes 3145732
  95.1 3.6 %copy-start.8 = (pred[512,512]{1,0:T(8,128)(4,1)S(1)}, pred[512,512]{1,0:T(8,128)(4,1)}, u32[]{:S(2)}) copy-start(pred[512,512]{1,0:T(8,128)(4,1)} %iota_compare_fusion) | copy-start | bytes 786436
  97.3 1.8 copy-start.3
  97.3 1.8 copy-start.5
  99.1 2.8 %slice-start.4 = ((f32[33,1024]{1,0:T(8,128)}), f32[32,1024]{1,0:T(8,128)S(1)}, s32[]{:S(2)}) async-start(f32[33,1024]{1,0:T(8,128)} %copy-done.6), calls=%async_computation.10 | async-start | bytes 262144 | tf_op jit(solution)/shard_map/slice | solution.py:150
  99.1 2.8 %copy-start.9 = (f32[32,2,512]{2,1,0:T(2,128)S(1)}, f32[32,2,512]{2,1,0:T(2,128)}, u32[]{:S(2)}) copy-start(f32[32,2,512]{2,1,0:T(2,128)} %slice.163) | copy-start | bytes 393220
  99.1 2.9 %copy-start.10 = (f32[2]{0:T(128)S(1)}, f32[2]{0:T(128)}, u32[]{:S(2)}) copy-start(f32[2]{0:T(128)} %constant.96.clone) | copy-start | bytes 28
  99.1 2.9 %copy-start.11 = (f32[2]{0:T(128)S(1)}, f32[2]{0:T(128)}, u32[]{:S(2)}) copy-start(f32[2]{0:T(128)} %constant.105) | copy-start | bytes 28
  102.2 13.3 %slice-start = ((s8[16777216]{0:T(1024)(128)(4,1)}), s8[4194304]{0:T(1024)(128)(4,1)S(1)}, s32[]{:S(2)}) async-start(s8[16777216]{0:T(1024)(128)(4,1)} %bitcast.190), calls=%async_computation.6 | async-start | bytes 8388608
  103.8 11.7 %slice-start.1 = ((s8[16777216]{0:T(1024)(128)(4,1)}), s8[4194304]{0:T(1024)(128)(4,1)S(1)}, s32[]{:S(2)}) async-start(s8[16777216]{0:T(1024)(128)(4,1)} %bitcast.190), calls=%async_computation.7 | async-start | bytes 8388608
  106.3 9.2 %slice-start.2 = ((s8[16777216]{0:T(1024)(128)(4,1)}), s8[4194304]{0:T(1024)(128)(4,1)S(1)}, s32[]{:S(2)}) async-start(s8[16777216]{0:T(1024)(128)(4,1)} %bitcast.190), calls=%async_computation.8 | async-start | bytes 8388608
  108.1 7.3 %slice-start.3 = ((s8[16777216]{0:T(1024)(128)(4,1)}), s8[4194304]{0:T(1024)(128)(4,1)S(1)}, s32[]{:S(2)}) async-start(s8[16777216]{0:T(1024)(128)(4,1)} %bitcast.190), calls=%async_computation.9 | async-start | bytes 8388608
  121.1 20.4 %all-to-all-start.5 = ((bf16[32,2,2,4096]{3,2,1,0:T(2,128)(2,1)}), bf16[32,2,2,4096]{3,2,1,0:T(2,128)(2,1)S(1)}, u32[]{:S(2)}, u32[]{:S(2)}) async-start(bf16[32,2,2,4096]{3,2,1,0:T(2,128)(2,1)} %copy.79), calls=%async_computation.5 | async-start | bytes 2097152 | tf_op jit(solution)/shard_map/all_to_all | solution.py:218
  141.5 19.4 %all-to-all-start.4 = ((bf16[32,2,2,4096]{3,2,1,0:T(2,128)(2,1)}), bf16[32,2,2,4096]{3,2,1,0:T(2,128)(2,1)S(1)}, u32[]{:S(2)}, u32[]{:S(2)}) async-start(bf16[32,2,2,4096]{3,2,1,0:T(2,128)(2,1)} %copy.77), calls=%async_computation.4 | async-start | bytes 2097152 | tf_op jit(solution)/shard_map/all_to_all | solution.py:218
  166.3 6.5 %collective-permute-start.1 = (f32[4,32,33]{2,1,0:T(8,128)S(1)}, f32[4,32,33]{2,1,0:T(8,128)S(1)}, u32[]{:S(2)}, u32[]{:S(2)}) collective-permute-start(f32[4,32,33]{2,1,0:T(8,128)S(1)} %pad_maximum_fusion.4), channel_id=1, source_target_pairs={{0,16},{8,24},{16,0},{24,8},{32,48},{40,56},{48,32},{56,40},{64,80... | collective-permute-start | bytes 50696 | tf_op jit(solution)/shard_map/ppermute | solution.py:79
  167.4 5.5 %collective-permute-start.2 = (f32[4,32,33]{2,1,0:T(8,128)S(1)}, f32[4,32,33]{2,1,0:T(8,128)S(1)}, u32[]{:S(2)}, u32[]{:S(2)}) collective-permute-start(f32[4,32,33]{2,1,0:T(8,128)S(1)} %pad_maximum_fusion.4), channel_id=1, source_target_pairs={{0,24},{8,0},{16,8},{24,16},{32,56},{40,32},{48,40},{56,48},{64,88... | collective-permute-start | bytes 50696 | tf_op jit(solution)/shard_map/ppermute | solution.py:79
  169.7 5.5 %collective-permute-start = (f32[4,32,33]{2,1,0:T(8,128)S(1)}, f32[4,32,33]{2,1,0:T(8,128)S(1)}, u32[]{:S(2)}, u32[]{:S(2)}) collective-permute-start(f32[4,32,33]{2,1,0:T(8,128)S(1)} %pad_maximum_fusion.4), channel_id=1, source_target_pairs={{0,8},{8,16},{16,24},{24,0},{32,40},{40,48},{48,56},{56,32},{64,72... | collective-permute-start | bytes 50696 | tf_op jit(solution)/shard_map/ppermute | solution.py:79
  175.2 4.3 %collective-permute-start.5 = (f32[4,32,33]{2,1,0:T(8,128)S(1)}, f32[4,32,33]{2,1,0:T(8,128)S(1)}, u32[]{:S(2)}, u32[]{:S(2)}) collective-permute-start(f32[4,32,33]{2,1,0:T(8,128)S(1)} %add_add_fusion.1), channel_id=1, source_target_pairs={{0,96},{8,104},{16,112},{24,120},{32,0},{40,8},{48,16},{56,24},{64... | collective-permute-start | bytes 50696 | tf_op jit(solution)/shard_map/ppermute | solution.py:79
  176.3 5.8 %collective-permute-start.4 = (f32[4,32,33]{2,1,0:T(8,128)S(1)}, f32[4,32,33]{2,1,0:T(8,128)S(1)}, u32[]{:S(2)}, u32[]{:S(2)}) collective-permute-start(f32[4,32,33]{2,1,0:T(8,128)S(1)} %add_add_fusion.1), channel_id=1, source_target_pairs={{0,64},{8,72},{16,80},{24,88},{32,96},{40,104},{48,112},{56,120},{... | collective-permute-start | bytes 50696 | tf_op jit(solution)/shard_map/ppermute | solution.py:79
  176.9 5.8 %collective-permute-start.3 = (f32[4,32,33]{2,1,0:T(8,128)S(1)}, f32[4,32,33]{2,1,0:T(8,128)S(1)}, u32[]{:S(2)}, u32[]{:S(2)}) collective-permute-start(f32[4,32,33]{2,1,0:T(8,128)S(1)} %add_add_fusion.1), channel_id=1, source_target_pairs={{0,32},{8,40},{16,48},{24,56},{32,64},{40,72},{48,80},{56,88},{64,... | collective-permute-start | bytes 50696 | tf_op jit(solution)/shard_map/ppermute | solution.py:79

commit v3 on v2

--- a/solution.py
+++ b/solution.py
@@ -192,7 +192,7 @@
     coef = chebyshev(times_system, stacked, low_edge, high_edge)
     scaled = (inv_scale[:, None, None, :] * coef).astype(jnp.bfloat16)
     offset = jnp.einsum(
-        "bi,brpi->pbr", mean_dose, scaled.astype(jnp.float32), precision=lax.Precision.HIGHEST
+        "bi,brpi->pbr", mean_dose, scaled.astype(jnp.float32), precision=lax.Precision.HIGH
     )
     halves = 2
     part_rows = sample_rows // halves
@@ -240,7 +240,7 @@
     weight = spd_solve(level_system, (hcross_out / held_rows)[:, :, None])[:, :, 0]
     return jnp.concatenate(
         [
-            jnp.einsum("pq,pqs->ps", weight, f.astype(jnp.float32), precision=lax.Precision.HIGHEST)
+            jnp.einsum("pq,pqs->ps", weight, f.astype(jnp.float32), precision=lax.Precision.HIGH)
             for f in level_parts
         ],
         axis=1,

time: 199 us -> 198 us (level)
  no operation moved by 1% of the time
where the time goes in v3:
time: 198 us; the launch traced here: 197 us
  waiting for transfers between devices  67.8 us (34%)
  matrix products  47.2 us (24%)
  starting transfers between devices  36.6 us (18%)
  local copies, waits for them, and re-layouts  19.8 us (10%)
  other arithmetic  14.8 us (7%)
  Pallas kernels  10.5 us (5%)
    all_to_all x2, waiting for transfers between devices, per_device(): lax.all_to_all(feature, 'blk', split_axis=0, concat_axis=1, tiled=True)  25.8 us
    dot_general x2, matrix products, per_device(): jnp.einsum('si,sj->ij', xb, xb, preferred_element_type=jnp.float32)  19.9 us
    all_to_all x2, waiting for transfers between devices, exchange_sum(): lax.all_to_all(jnp.broadcast_to(chunk[None], (n,) + chunk.shape), axis, 0...  18.3 us
    all_to_all x2, starting transfers between devices, exchange_sum(): pieces = lax.all_to_all(flat.reshape(n, -1, 128), axis, 0, 0, tiled=True)  15.2 us
    all_to_all x2, waiting for transfers between devices, exchange_sum(): pieces = lax.all_to_all(flat.reshape(n, -1, 128), axis, 0, 0, tiled=True)  13 us
    ppermute x6, waiting for transfers between devices, butterfly_sum(): total = total + lax.ppermute(x, axis, perm)  10.7 us
    pallas_call x1, Pallas kernels, spd_solve(): pl.pallas_call(_spd_solve_kernel, out_shape=jax.ShapeDtypeStruct(b.shape,...  10.5 us
    dot_general x4, matrix products, per_device(): jnp.einsum('si,rpi->prs', genotypes[rows_h, b * B:(b + 1) * B], scaled[b]...  10.1 us
  transfers between devices with their start and end apart: 12, of which 10 were waited for; matrix products, arithmetic and copies ran while one was open for 16% of the time, Pallas kernels for 0%

profile of v3, /device:TPU:0, one launch (start us, length us, event | category | flops | bytes accessed | tf_op | source)
XLA Modules:
  0.0 197.5 jit_solution(3002894307608929837)
XLA Ops:
  0.0 9.9 %fusion.2 = f32[512,512]{1,0:T(8,128)S(1)} fusion(bf16[8192,1024]{1,0:T(8,128)(2,1)} %param.6), kind=kOutput, calls=%fused_computation.3 | convolution fusion | flops 4294967296 | bytes 9437184 | tf_op jit(solution)/shard_map/si,sj->ij/dot_general | solution.py:135
  12.0 8.0 %all-to-all-start = ((f32[16,72,128]{2,1,0:T(8,128)}), f32[16,72,128]{2,1,0:T(8,128)S(1)}, u32[]{:S(2)}, u32[]{:S(2)}) async-start(f32[16,72,128]{2,1,0:T(8,128)} %bitcast.1), calls=%async_computation | async-start | bytes 1179648 | tf_op jit(solution)/shard_map/all_to_all | solution.py:91
  20.6 10.0 %fusion = f32[512,512]{1,0:T(8,128)S(1)} fusion(bf16[8192,1024]{1,0:T(8,128)(2,1)} %param.6), kind=kOutput, calls=%fused_computation.1 | convolution fusion | flops 4294967296 | bytes 9437184 | tf_op jit(solution)/shard_map/si,sj->ij/dot_general | solution.py:135
  31.9 8.7 %fusion.91 = f32[33,1024]{1,0:T(8,128)S(1)} fusion(bf16[8192,1024]{1,0:T(8,128)(2,1)} %param.6, bf16[32,8192]{1,0:T(8,128)(2,1)S(1)} %get-tuple-element.20), kind=kOutput, calls=%fused_computation.73 | convolution fusion | flops 553648128 | bytes 17436672 | tf_op jit(solution)/shard_map/dot_general | solution.py:139
  42.5 7.2 %all-to-all-start.2 = ((f32[16,88,128]{2,1,0:T(8,128)}), f32[16,88,128]{2,1,0:T(8,128)S(1)}, u32[]{:S(2)}, u32[]{:S(2)}) async-start(f32[16,88,128]{2,1,0:T(8,128)} %bitcast.8), calls=%async_computation.2 | async-start | bytes 1441792 | tf_op jit(solution)/shard_map/all_to_all | solution.py:91
  49.8 13.0 %all-to-all-done.2 = f32[16,88,128]{2,1,0:T(8,128)S(1)} async-done(((f32[16,88,128]{2,1,0:T(8,128)}), f32[16,88,128]{2,1,0:T(8,128)S(1)}, u32[]{:S(2)}, u32[]{:S(2)}) %all-to-all-start.2) | async-done | bytes 720928 | tf_op jit(solution)/shard_map/all_to_all | solution.py:91
  63.7 3.7 %all-to-all-start.1 = ((f32[16,72,128]{2,1,0:T(8,128)}), f32[16,72,128]{2,1,0:T(8,128)S(1)}, u32[]{:S(2)}, u32[]{:S(2)}) async-start(f32[16,72,128]{2,1,0:T(8,128)} %broadcast_in_dim.113), calls=%async_computation.1 | async-start | bytes 1179648 | tf_op jit(solution)/shard_map/all_to_all | solution.py:93
  67.4 10.8 %all-to-all-done.1 = f32[16,72,128]{2,1,0:T(8,128)S(1)} async-done(((f32[16,72,128]{2,1,0:T(8,128)}), f32[16,72,128]{2,1,0:T(8,128)S(1)}, u32[]{:S(2)}, u32[]{:S(2)}) %all-to-all-start.1) | async-done | bytes 589856 | tf_op jit(solution)/shard_map/all_to_all | solution.py:93
  79.1 3.8 %all-to-all-start.3 = ((f32[16,88,128]{2,1,0:T(8,128)}), f32[16,88,128]{2,1,0:T(8,128)S(1)}, u32[]{:S(2)}, u32[]{:S(2)}) async-start(f32[16,88,128]{2,1,0:T(8,128)} %broadcast_in_dim.119), calls=%async_computation.3 | async-start | bytes 1441792 | tf_op jit(solution)/shard_map/all_to_all | solution.py:93
  86.3 7.6 %all-to-all-done.3 = f32[16,88,128]{2,1,0:T(8,128)S(1)} async-done(((f32[16,88,128]{2,1,0:T(8,128)}), f32[16,88,128]{2,1,0:T(8,128)S(1)}, u32[]{:S(2)}, u32[]{:S(2)}) %all-to-all-start.3) | async-done | bytes 720928 | tf_op jit(solution)/shard_map/all_to_all | solution.py:93
  97.3 1.3 maximum_bitcast_fusion.1
  99.1 2.6 %abs_reduce_fusion = (f32[2,512]{1,0:T(2,128)S(1)}, f32[2,512,512]{2,1,0:T(8,128)S(1)}) fusion(f32[2,512]{1,0:T(2,128)S(1)} %get-tuple-element.37, f32[2,512]{1,0:T(2,128)S(1)} %get-tuple-element.38, f32[2,512]{1,0:T(2,128)S(1)} %get-tuple-element.39, f32[2,512]{1,0:T(2,128)S(1)} %get-tuple-element.40, f32[1,512,512]{2,1,0:T(8,128)S(1)} %bitcast.201, ...), kind=kLoop, calls=%fused_computation.43 | loop fusion | flops 7339008 | bytes 6311936 | tf_op jit(solution)/shard_map/reduce_sum | solution.py:174
  108.2 3.7 %convolution_bitcast_fusion = f32[32,1,2,4096]{3,0,2,1:T(8,128)S(1)} fusion(bf16[8192,1024]{1,0:T(8,128)(2,1)} %param.6, bf16[2,2,32,512]{3,2,1,0:T(8,128)(2,1)S(1)} %fusion.88), kind=kOutput, calls=%fused_computation.5 | convolution fusion | flops 268435456 | bytes 5308416 | tf_op jit(solution)/shard_map/si,rpi->prs/dot_general | solution.py:207
  111.9 3.6 %convolution_bitcast_fusion.1 = f32[32,1,2,4096]{3,0,2,1:T(8,128)S(1)} fusion(bf16[8192,1024]{1,0:T(8,128)(2,1)} %param.6, bf16[2,2,32,512]{3,2,1,0:T(8,128)(2,1)S(1)} %fusion.88), kind=kOutput, calls=%fused_computation.6 | convolution fusion | flops 268435456 | bytes 5308416 | tf_op jit(solution)/shard_map/si,rpi->prs/dot_general | solution.py:207
  115.5 1.4 convolution_bitcast_fusion.2
  116.9 1.4 convolution_bitcast_fusion.3
  119.0 2.1 %copy.79 = bf16[32,2,2,4096]{3,2,1,0:T(2,128)(2,1)} copy(bf16[32,2,2,4096]{3,0,2,1:T(8,128)(2,1)S(1)} %get-tuple-element.41) | data formatting | bytes 2097152 | tf_op jit(solution)/shard_map/convert_element_type | solution.py:217
  121.0 4.5 %all-to-all-start.5 = ((bf16[32,2,2,4096]{3,2,1,0:T(2,128)(2,1)}), bf16[32,2,2,4096]{3,2,1,0:T(2,128)(2,1)S(1)}, u32[]{:S(2)}, u32[]{:S(2)}) async-start(bf16[32,2,2,4096]{3,2,1,0:T(2,128)(2,1)} %copy.79), calls=%async_computation.5 | async-start | bytes 2097152 | tf_op jit(solution)/shard_map/all_to_all | solution.py:218
  125.5 2.1 %copy.77 = bf16[32,2,2,4096]{3,2,1,0:T(2,128)(2,1)} copy(bf16[32,2,2,4096]{3,0,2,1:T(8,128)(2,1)S(1)} %get-tuple-element.42) | data formatting | bytes 2097152 | tf_op jit(solution)/shard_map/convert_element_type | solution.py:217
  127.6 13.9 %all-to-all-done.5 = bf16[32,2,2,4096]{3,2,1,0:T(2,128)(2,1)S(1)} async-done(((bf16[32,2,2,4096]{3,2,1,0:T(2,128)(2,1)}), bf16[32,2,2,4096]{3,2,1,0:T(2,128)(2,1)S(1)}, u32[]{:S(2)}, u32[]{:S(2)}) %all-to-all-start.5) | async-done | bytes 1048608 | tf_op jit(solution)/shard_map/all_to_all | solution.py:218
  141.4 3.8 %all-to-all-start.4 = ((bf16[32,2,2,4096]{3,2,1,0:T(2,128)(2,1)}), bf16[32,2,2,4096]{3,2,1,0:T(2,128)(2,1)S(1)}, u32[]{:S(2)}, u32[]{:S(2)}) async-start(bf16[32,2,2,4096]{3,2,1,0:T(2,128)(2,1)} %copy.77), calls=%async_computation.4 | async-start | bytes 2097152 | tf_op jit(solution)/shard_map/all_to_all | solution.py:218
  145.3 2.1 %copy.108 = bf16[8,4,2,2,4096]{4,3,2,0,1:T(2,128)(2,1)} copy(bf16[8,4,2,2,4096]{4,3,2,1,0:T(2,128)(2,1)S(1)} %bitcast.192) | data formatting | bytes 2097152 | tf_op jit(solution)/shard_map/all_to_all | solution.py:218
  147.4 1.5 reshape.899
  148.9 11.9 %all-to-all-done.4 = bf16[32,2,2,4096]{3,2,1,0:T(2,128)(2,1)S(1)} async-done(((bf16[32,2,2,4096]{3,2,1,0:T(2,128)(2,1)}), bf16[32,2,2,4096]{3,2,1,0:T(2,128)(2,1)S(1)}, u32[]{:S(2)}, u32[]{:S(2)}) %all-to-all-start.4) | async-done | bytes 1048608 | tf_op jit(solution)/shard_map/all_to_all | solution.py:218
  160.9 2.1 %copy.109 = bf16[8,4,2,2,4096]{4,3,2,0,1:T(2,128)(2,1)} copy(bf16[8,4,2,2,4096]{4,3,2,1,0:T(2,128)(2,1)S(1)} %bitcast.193) | data formatting | bytes 2097152 | tf_op jit(solution)/shard_map/all_to_all | solution.py:218
  163.0 1.5 reshape.898
  167.3 2.3 %collective-permute-start.2 = (f32[4,32,33]{2,1,0:T(8,128)S(1)}, f32[4,32,33]{2,1,0:T(8,128)S(1)}, u32[]{:S(2)}, u32[]{:S(2)}) collective-permute-start(f32[4,32,33]{2,1,0:T(8,128)S(1)} %pad_maximum_fusion.4), channel_id=1, source_target_pairs={{0,24},{8,0},{16,8},{24,16},{32,56},{40,32},{48,40},{56,48},{64,88... | collective-permute-start | bytes 50696 | tf_op jit(solution)/shard_map/ppermute | solution.py:79
  169.6 3.2 %collective-permute-done.1 = f32[4,32,33]{2,1,0:T(8,128)S(1)} collective-permute-done((f32[4,32,33]{2,1,0:T(8,128)S(1)}, f32[4,32,33]{2,1,0:T(8,128)S(1)}, u32[]{:S(2)}, u32[]{:S(2)}) %collective-permute-start.1) | collective-permute-done | bytes 16928 | tf_op jit(solution)/shard_map/ppermute | solution.py:79
  172.8 2.3 %collective-permute-done = f32[4,32,33]{2,1,0:T(8,128)S(1)} collective-permute-done((f32[4,32,33]{2,1,0:T(8,128)S(1)}, f32[4,32,33]{2,1,0:T(8,128)S(1)}, u32[]{:S(2)}, u32[]{:S(2)}) %collective-permute-start) | collective-permute-done | bytes 16928 | tf_op jit(solution)/shard_map/ppermute | solution.py:79
  177.4 2.0 %collective-permute-done.5 = f32[4,32,33]{2,1,0:T(8,128)S(1)} collective-permute-done((f32[4,32,33]{2,1,0:T(8,128)S(1)}, f32[4,32,33]{2,1,0:T(8,128)S(1)}, u32[]{:S(2)}, u32[]{:S(2)}) %collective-permute-start.5) | collective-permute-done | bytes 16928 | tf_op jit(solution)/shard_map/ppermute | solution.py:79
  179.5 2.5 %collective-permute-done.4 = f32[4,32,33]{2,1,0:T(8,128)S(1)} collective-permute-done((f32[4,32,33]{2,1,0:T(8,128)S(1)}, f32[4,32,33]{2,1,0:T(8,128)S(1)}, u32[]{:S(2)}, u32[]{:S(2)}) %collective-permute-start.4) | collective-permute-done | bytes 16928 | tf_op jit(solution)/shard_map/ppermute | solution.py:79
  184.4 10.5 %shard_map.46 = f32[4,32,1]{2,1,0:T(8,128)} custom-call(f32[4,32,32]{2,1,0:T(8,128)} %multiply_add_fusion.11.a_ref, f32[4,32,1]{2,1,0:T(8,128)} %copy.82.b_ref), custom_call_target="tpu_custom_call" | custom-call | tf_op jit(solution)/shard_map/pallas_call | solution.py:60
  (128 shorter events, 31.8 us)
Async XLA Ops:
  0.0 30.7 %copy-start = (bf16[32,8192]{1,0:T(8,128)(2,1)S(1)}, bf16[32,8192]{1,0:T(8,128)(2,1)}, u32[]{:S(2)}) copy-start(bf16[32,8192]{1,0:T(8,128)(2,1)} %param.7) | copy-start | bytes 1572868
  9.9 1.0 copy-start.2
  11.0 9.6 %copy-start.12 = (s32[32]{0:T(128)S(1)}, s32[32]{0:T(128)}, u32[]{:S(2)}) copy-start(s32[32]{0:T(128)} %param.8) | copy-start | bytes 388
  12.0 30.6 %all-to-all-start = ((f32[16,72,128]{2,1,0:T(8,128)}), f32[16,72,128]{2,1,0:T(8,128)S(1)}, u32[]{:S(2)}, u32[]{:S(2)}) async-start(f32[16,72,128]{2,1,0:T(8,128)} %bitcast.1), calls=%async_computation | async-start | bytes 1179648 | tf_op jit(solution)/shard_map/all_to_all | solution.py:91
  30.6 10.8 %copy-start.4 = (f32[512,512]{1,0:T(8,128)}, f32[512,512]{1,0:T(8,128)S(1)}, u32[]{:S(2)}) copy-start(f32[512,512]{1,0:T(8,128)S(1)} %fusion) | copy-start | bytes 3145732
  40.6 0.7 copy-start.6
  42.5 20.3 %all-to-all-start.2 = ((f32[16,88,128]{2,1,0:T(8,128)}), f32[16,88,128]{2,1,0:T(8,128)S(1)}, u32[]{:S(2)}, u32[]{:S(2)}) async-start(f32[16,88,128]{2,1,0:T(8,128)} %bitcast.8), calls=%async_computation.2 | async-start | bytes 1441792 | tf_op jit(solution)/shard_map/all_to_all | solution.py:91
  63.7 19.3 %copy-start.7 = (f32[33,1024]{1,0:T(8,128)S(1)}, f32[33,1024]{1,0:T(8,128)}, u32[]{:S(2)}) copy-start(f32[33,1024]{1,0:T(8,128)} %copy-done.6) | copy-start | bytes 405508
  63.7 14.5 %all-to-all-start.1 = ((f32[16,72,128]{2,1,0:T(8,128)}), f32[16,72,128]{2,1,0:T(8,128)S(1)}, u32[]{:S(2)}, u32[]{:S(2)}) async-start(f32[16,72,128]{2,1,0:T(8,128)} %broadcast_in_dim.113), calls=%async_computation.1 | async-start | bytes 1179648 | tf_op jit(solution)/shard_map/all_to_all | solution.py:93
  79.1 14.8 %all-to-all-start.3 = ((f32[16,88,128]{2,1,0:T(8,128)}), f32[16,88,128]{2,1,0:T(8,128)S(1)}, u32[]{:S(2)}, u32[]{:S(2)}) async-start(f32[16,88,128]{2,1,0:T(8,128)} %broadcast_in_dim.119), calls=%async_computation.3 | async-start | bytes 1441792 | tf_op jit(solution)/shard_map/all_to_all | solution.py:93
  86.3 12.3 %copy-start.1 = (f32[1,512,512]{2,1,0:T(8,128)}, f32[1,512,512]{2,1,0:T(8,128)S(1)}, u32[]{:S(2)}) copy-start(f32[1,512,512]{2,1,0:T(8,128)S(1)} %maximum_bitcast_fusion) | copy-start | bytes 3145732
  95.1 3.6 %copy-start.8 = (pred[512,512]{1,0:T(8,128)(4,1)S(1)}, pred[512,512]{1,0:T(8,128)(4,1)}, u32[]{:S(2)}) copy-start(pred[512,512]{1,0:T(8,128)(4,1)} %iota_compare_fusion) | copy-start | bytes 786436
  97.3 1.8 copy-start.3
  97.3 1.8 copy-start.5
  99.1 2.8 %slice-start.4 = ((f32[33,1024]{1,0:T(8,128)}), f32[32,1024]{1,0:T(8,128)S(1)}, s32[]{:S(2)}) async-start(f32[33,1024]{1,0:T(8,128)} %copy-done.6), calls=%async_computation.10 | async-start | bytes 262144 | tf_op jit(solution)/shard_map/slice | solution.py:150
  99.1 2.8 %copy-start.9 = (f32[32,2,512]{2,1,0:T(2,128)S(1)}, f32[32,2,512]{2,1,0:T(2,128)}, u32[]{:S(2)}) copy-start(f32[32,2,512]{2,1,0:T(2,128)} %slice.163) | copy-start | bytes 393220
  99.1 2.9 %copy-start.10 = (f32[2]{0:T(128)S(1)}, f32[2]{0:T(128)}, u32[]{:S(2)}) copy-start(f32[2]{0:T(128)} %constant.96.clone) | copy-start | bytes 28
  99.1 2.9 %copy-start.11 = (f32[2]{0:T(128)S(1)}, f32[2]{0:T(128)}, u32[]{:S(2)}) copy-start(f32[2]{0:T(128)} %constant.105) | copy-start | bytes 28
  102.2 13.3 %slice-start = ((s8[16777216]{0:T(1024)(128)(4,1)}), s8[4194304]{0:T(1024)(128)(4,1)S(1)}, s32[]{:S(2)}) async-start(s8[16777216]{0:T(1024)(128)(4,1)} %bitcast.190), calls=%async_computation.6 | async-start | bytes 8388608
  103.8 11.7 %slice-start.1 = ((s8[16777216]{0:T(1024)(128)(4,1)}), s8[4194304]{0:T(1024)(128)(4,1)S(1)}, s32[]{:S(2)}) async-start(s8[16777216]{0:T(1024)(128)(4,1)} %bitcast.190), calls=%async_computation.7 | async-start | bytes 8388608
  106.3 9.2 %slice-start.2 = ((s8[16777216]{0:T(1024)(128)(4,1)}), s8[4194304]{0:T(1024)(128)(4,1)S(1)}, s32[]{:S(2)}) async-start(s8[16777216]{0:T(1024)(128)(4,1)} %bitcast.190), calls=%async_computation.8 | async-start | bytes 8388608
  108.1 7.3 %slice-start.3 = ((s8[16777216]{0:T(1024)(128)(4,1)}), s8[4194304]{0:T(1024)(128)(4,1)S(1)}, s32[]{:S(2)}) async-start(s8[16777216]{0:T(1024)(128)(4,1)} %bitcast.190), calls=%async_computation.9 | async-start | bytes 8388608
  121.0 20.4 %all-to-all-start.5 = ((bf16[32,2,2,4096]{3,2,1,0:T(2,128)(2,1)}), bf16[32,2,2,4096]{3,2,1,0:T(2,128)(2,1)S(1)}, u32[]{:S(2)}, u32[]{:S(2)}) async-start(bf16[32,2,2,4096]{3,2,1,0:T(2,128)(2,1)} %copy.79), calls=%async_computation.5 | async-start | bytes 2097152 | tf_op jit(solution)/shard_map/all_to_all | solution.py:218
  141.4 19.4 %all-to-all-start.4 = ((bf16[32,2,2,4096]{3,2,1,0:T(2,128)(2,1)}), bf16[32,2,2,4096]{3,2,1,0:T(2,128)(2,1)S(1)}, u32[]{:S(2)}, u32[]{:S(2)}) async-start(bf16[32,2,2,4096]{3,2,1,0:T(2,128)(2,1)} %copy.77), calls=%async_computation.4 | async-start | bytes 2097152 | tf_op jit(solution)/shard_map/all_to_all | solution.py:218
  166.3 6.5 %collective-permute-start.1 = (f32[4,32,33]{2,1,0:T(8,128)S(1)}, f32[4,32,33]{2,1,0:T(8,128)S(1)}, u32[]{:S(2)}, u32[]{:S(2)}) collective-permute-start(f32[4,32,33]{2,1,0:T(8,128)S(1)} %pad_maximum_fusion.4), channel_id=1, source_target_pairs={{0,16},{8,24},{16,0},{24,8},{32,48},{40,56},{48,32},{56,40},{64,80... | collective-permute-start | bytes 50696 | tf_op jit(solution)/shard_map/ppermute | solution.py:79
  167.3 5.5 %collective-permute-start.2 = (f32[4,32,33]{2,1,0:T(8,128)S(1)}, f32[4,32,33]{2,1,0:T(8,128)S(1)}, u32[]{:S(2)}, u32[]{:S(2)}) collective-permute-start(f32[4,32,33]{2,1,0:T(8,128)S(1)} %pad_maximum_fusion.4), channel_id=1, source_target_pairs={{0,24},{8,0},{16,8},{24,16},{32,56},{40,32},{48,40},{56,48},{64,88... | collective-permute-start | bytes 50696 | tf_op jit(solution)/shard_map/ppermute | solution.py:79
  169.6 5.5 %collective-permute-start = (f32[4,32,33]{2,1,0:T(8,128)S(1)}, f32[4,32,33]{2,1,0:T(8,128)S(1)}, u32[]{:S(2)}, u32[]{:S(2)}) collective-permute-start(f32[4,32,33]{2,1,0:T(8,128)S(1)} %pad_maximum_fusion.4), channel_id=1, source_target_pairs={{0,8},{8,16},{16,24},{24,0},{32,40},{40,48},{48,56},{56,32},{64,72... | collective-permute-start | bytes 50696 | tf_op jit(solution)/shard_map/ppermute | solution.py:79
  175.2 4.3 %collective-permute-start.5 = (f32[4,32,33]{2,1,0:T(8,128)S(1)}, f32[4,32,33]{2,1,0:T(8,128)S(1)}, u32[]{:S(2)}, u32[]{:S(2)}) collective-permute-start(f32[4,32,33]{2,1,0:T(8,128)S(1)} %add_add_fusion.1), channel_id=1, source_target_pairs={{0,96},{8,104},{16,112},{24,120},{32,0},{40,8},{48,16},{56,24},{64... | collective-permute-start | bytes 50696 | tf_op jit(solution)/shard_map/ppermute | solution.py:79
  176.2 5.8 %collective-permute-start.4 = (f32[4,32,33]{2,1,0:T(8,128)S(1)}, f32[4,32,33]{2,1,0:T(8,128)S(1)}, u32[]{:S(2)}, u32[]{:S(2)}) collective-permute-start(f32[4,32,33]{2,1,0:T(8,128)S(1)} %add_add_fusion.1), channel_id=1, source_target_pairs={{0,64},{8,72},{16,80},{24,88},{32,96},{40,104},{48,112},{56,120},{... | collective-permute-start | bytes 50696 | tf_op jit(solution)/shard_map/ppermute | solution.py:79
  176.8 5.8 %collective-permute-start.3 = (f32[4,32,33]{2,1,0:T(8,128)S(1)}, f32[4,32,33]{2,1,0:T(8,128)S(1)}, u32[]{:S(2)}, u32[]{:S(2)}) collective-permute-start(f32[4,32,33]{2,1,0:T(8,128)S(1)} %add_add_fusion.1), channel_id=1, source_target_pairs={{0,32},{8,40},{16,48},{24,56},{32,64},{40,72},{48,80},{56,88},{64,... | collective-permute-start | bytes 50696 | tf_op jit(solution)/shard_map/ppermute | solution.py:79
